TPU v7x, 128 devices: a whole 4x4x4 slice. The times are simulated.
128 devices in a mesh: dp: 2 (over core), seq: 16 (over z, x), head: 4 (over y).
Axes of the slice: x: 4, y: 4, z: 4, core: 2. Of those that a mesh axis runs over, the one named last changes fastest.
Arguments:
- queries: bfloat16 [2, 10240, 2048], P('dp', ('seq', 'head')), may hold values from -45 to 45
- key_rows: bfloat16 [2, 10240, 2048], P('dp', ('seq', 'head')), may hold values from -6 to 6
- values: bfloat16 [2, 10240, 2048], P('dp', ('seq', 'head')), may hold values from -6 to 6
- rand_blocks: int32 [160, 16, 4], P('seq', 'head'), may hold values from 0 to 159, as said below
- out_weight: bfloat16 [2048, 2048], P('head'), may hold values from -0.125 to 0.125
- cotangent: bfloat16 [2, 10240, 2048], P('dp', ('seq', 'head')), may hold values from -6 to 6
Outputs:
- layer_out: bfloat16 [2, 10240, 2048], P('dp', ('seq', 'head'))
- grad_queries: bfloat16 [2, 10240, 2048], P('dp', ('seq', 'head'))
- grad_keys: bfloat16 [2, 10240, 2048], P('dp', ('seq', 'head'))
- grad_values: bfloat16 [2, 10240, 2048], P('dp', ('seq', 'head'))
- weight_grad: float32 [2048, 2048], P('head')
Inputs may be any that keep to these rules, and one draw needn't show every extreme that they name: `rand_blocks`: key block b lies in range b // 10 of seq. Over the 10 query blocks of one index of seq and the 4 heads of one index of head, at most 15 of the listed random blocks lie in any one range of seq; in every draw, for every index of head, some range of seq receives exactly 15 of them from every index of seq.
All inputs are finite; a program needn't handle non-finite values.
Results may differ from a plain program's by a relative error of at most 0.034.
Values may be sent and summed in bfloat16 or wider, within the bound.
No kernel may reach another device: no remote copies, remote signals or barrier semaphores. Data moves between devices by JAX's collectives and lax.ppermute only.
A program may use at most 192 MiB of HBM per device.

v0:
```python
import math

import jax
import jax.numpy as jnp
from jax import lax
from jax.sharding import PartitionSpec as P

HEAD_SIZE = 128
BLOCK_TOKENS = 64


def with_halo(block, sides, width):
    for axis, dim in sides:
        count = lax.axis_size(axis)
        forward = [(i, i + 1) for i in range(count - 1)]
        backward = [(target, source) for source, target in forward]
        low = lax.ppermute(
            lax.slice_in_dim(block, block.shape[dim] - width, None, axis=dim), axis, forward
        )
        high = lax.ppermute(lax.slice_in_dim(block, 0, width, axis=dim), axis, backward)
        block = jnp.concatenate([low, block, high], axis=dim)
    return block


def from_root(block, axis, holder):
    block = jnp.where(lax.axis_index(axis) == holder, block, jnp.zeros_like(block))
    return lax.psum(block, axis)


def per_device(queries, key_rows, values, rand_blocks, out_weight, cotangent):
    block_len = BLOCK_TOKENS
    head_dim = HEAD_SIZE
    seq_count = lax.axis_size("seq")
    seq_index = lax.axis_index("seq")
    q_heads, k_heads, v_heads = (
        lax.all_to_all(queries, "head", split_axis=2, concat_axis=1, tiled=True),
        lax.all_to_all(key_rows, "head", split_axis=2, concat_axis=1, tiled=True),
        lax.all_to_all(values, "head", split_axis=2, concat_axis=1, tiled=True),
    )
    q_rows = q_heads[0]
    shard_len = q_rows.shape[0]
    width_cols = q_rows.shape[1]
    head_count = width_cols // head_dim
    block_count = shard_len // block_len
    rand_count = rand_blocks.shape[2]
    key_value = jnp.concatenate([k_heads[0], v_heads[0]], axis=1)
    padded = with_halo(key_value, (("seq", 0),), block_len)
    first_block = from_root(key_value[:block_len], "seq", 0)
    requests = jnp.transpose(rand_blocks, (0, 2, 1)).reshape(-1)
    request_count = requests.shape[0]
    head_of = jnp.arange(request_count, dtype=jnp.int32) % head_count
    capacity = 3 * request_count // (2 * seq_count)
    owners = requests // block_count
    offsets = requests % block_count
    one_hot = (owners[:, None] == jnp.arange(seq_count, dtype=jnp.int32)[None, :]).astype(jnp.int32)
    position = jnp.sum(one_hot * (jnp.cumsum(one_hot, axis=0) - 1), axis=1)
    slot_of = owners * capacity + position
    asked_codes = (
        jnp.full((seq_count * capacity,), -1, jnp.int32)
        .at[slot_of]
        .set(offsets * head_count + head_of)
        .reshape(seq_count, capacity)
    )
    asked_here = lax.all_to_all(asked_codes, "seq", split_axis=0, concat_axis=0, tiled=True)
    is_valid = asked_here >= 0
    asked_block = jnp.maximum(asked_here, 0) // head_count
    asked_head = jnp.maximum(asked_here, 0) % head_count
    block_view = key_value.reshape(block_count, block_len, 2, head_count, head_dim)
    served = block_view[asked_block, :, :, asked_head, :]
    served = jnp.where(is_valid[:, :, None, None, None], served, jnp.zeros_like(served))
    served = served.reshape(seq_count, capacity, block_len, 2 * head_dim)
    received = lax.all_to_all(served, "seq", split_axis=0, concat_axis=0, tiled=True)
    far_pairs = received.reshape(seq_count * capacity, block_len, 2, head_dim)[slot_of]
    pair_view = padded.reshape(block_count + 2, block_len, 2, head_count, head_dim)
    window_pairs = jnp.stack(
        [pair_view[:block_count], pair_view[1 : block_count + 1], pair_view[2:]], axis=1
    ).reshape(block_count, 3 * block_len, 2, head_count, head_dim)
    window_keys = window_pairs[:, :, 0]
    window_vals = window_pairs[:, :, 1]
    first_pairs = first_block.reshape(block_len, 2, head_count, head_dim)
    first_keys = first_pairs[:, 0]
    first_vals = first_pairs[:, 1]
    far_view = far_pairs.reshape(block_count, rand_count, head_count, block_len, 2, head_dim)
    far_keys = far_view[:, :, :, :, 0]
    far_vals = far_view[:, :, :, :, 1]
    global_ids = seq_index * block_count + jnp.arange(block_count, dtype=jnp.int32)
    block_total = seq_count * block_count
    window_live = jnp.stack([global_ids > 0, global_ids >= 0, global_ids < block_total - 1], axis=1)
    window_mask = jnp.repeat(window_live, block_len, axis=1)[None, :, None, :]
    query_blocks = q_rows.reshape(block_count, block_len, head_count, head_dim)
    softmax_scale = 1.0 / math.sqrt(head_dim)
    score_window = (
        jnp.einsum("ibhd,ikhd->hibk", query_blocks, window_keys, preferred_element_type=jnp.float32)
        * softmax_scale
    )
    score_first = (
        jnp.einsum("ibhd,khd->hibk", query_blocks, first_keys, preferred_element_type=jnp.float32)
        * softmax_scale
    )
    score_far = (
        jnp.einsum("ibhd,irhtd->hibrt", query_blocks, far_keys, preferred_element_type=jnp.float32)
        * softmax_scale
    )
    max_window = jnp.max(jnp.where(window_mask, score_window, -jnp.inf), axis=-1, keepdims=True)
    max_first = jnp.max(score_first, axis=-1, keepdims=True)
    max_far = jnp.max(score_far, axis=(-2, -1))[..., None]
    row_max = jnp.maximum(jnp.maximum(max_window, max_first), max_far)
    weight_window = jnp.where(window_mask, jnp.exp(score_window - row_max), 0.0)
    weight_first = jnp.exp(score_first - row_max)
    weight_far = jnp.exp(score_far - row_max[..., None])
    totals = (
        jnp.sum(weight_window, axis=-1, keepdims=True)
        + jnp.sum(weight_first, axis=-1, keepdims=True)
        + jnp.sum(weight_far, axis=(-2, -1))[..., None]
    )
    mixed = jnp.einsum(
        "hibk,ikhd->ibhd",
        weight_window.astype(jnp.bfloat16),
        window_vals,
        preferred_element_type=jnp.float32,
    )
    mixed = mixed + jnp.einsum(
        "hibk,khd->ibhd",
        weight_first.astype(jnp.bfloat16),
        first_vals,
        preferred_element_type=jnp.float32,
    )
    mixed = mixed + jnp.einsum(
        "hibrt,irhtd->ibhd",
        weight_far.astype(jnp.bfloat16),
        far_vals,
        preferred_element_type=jnp.float32,
    )
    totals_rows = jnp.transpose(totals, (1, 2, 0, 3))
    attn = (mixed / totals_rows).astype(jnp.bfloat16)
    logsum = row_max + jnp.log(totals)
    attn_rows = attn.reshape(shard_len, width_cols)
    layer_out = lax.psum_scatter(
        jnp.dot(attn_rows, out_weight, preferred_element_type=jnp.float32),
        "head",
        scatter_dimension=0,
        tiled=True,
    ).astype(jnp.bfloat16)[None]
    piece_flat = lax.all_gather(cotangent, "head", axis=1, tiled=True)[0]
    grad_piece = jnp.dot(piece_flat, out_weight.T, preferred_element_type=jnp.float32).astype(
        jnp.bfloat16
    )
    weight_acc = jnp.dot(attn_rows.T, piece_flat, preferred_element_type=jnp.float32)
    token_total = lax.axis_size("dp") * seq_count * shard_len
    weight_grad = lax.psum(weight_acc, ("dp", "seq")) * (1.0 / math.sqrt(token_total))
    grad_blocks = grad_piece.reshape(block_count, block_len, head_count, head_dim)
    delta_rows = jnp.sum(grad_blocks.astype(jnp.float32) * attn.astype(jnp.float32), axis=-1)
    row_delta = jnp.transpose(delta_rows, (2, 0, 1))[..., None]
    prob_window = jnp.where(window_mask, jnp.exp(score_window - logsum), 0.0)
    prob_first = jnp.exp(score_first - logsum)
    prob_far = jnp.exp(score_far - logsum[..., None])
    dprob_window = jnp.einsum(
        "ibhd,ikhd->hibk", grad_blocks, window_vals, preferred_element_type=jnp.float32
    )
    dprob_first = jnp.einsum(
        "ibhd,khd->hibk", grad_blocks, first_vals, preferred_element_type=jnp.float32
    )
    dprob_far = jnp.einsum(
        "ibhd,irhtd->hibrt", grad_blocks, far_vals, preferred_element_type=jnp.float32
    )
    dscore_window = (prob_window * (dprob_window - row_delta)).astype(jnp.bfloat16)
    dscore_first = (prob_first * (dprob_first - row_delta)).astype(jnp.bfloat16)
    dscore_far = (prob_far * (dprob_far - row_delta[..., None])).astype(jnp.bfloat16)
    grad_q = jnp.einsum(
        "hibk,ikhd->ibhd", dscore_window, window_keys, preferred_element_type=jnp.float32
    )
    grad_q = grad_q + jnp.einsum(
        "hibk,khd->ibhd", dscore_first, first_keys, preferred_element_type=jnp.float32
    )
    grad_q = grad_q + jnp.einsum(
        "hibrt,irhtd->ibhd", dscore_far, far_keys, preferred_element_type=jnp.float32
    )
    grad_q = (grad_q * softmax_scale).astype(jnp.bfloat16)
    key_window = (
        jnp.einsum(
            "hibk,ibhd->ikhd", dscore_window, query_blocks, preferred_element_type=jnp.float32
        )
        * softmax_scale
    )
    value_window = jnp.einsum(
        "hibk,ibhd->ikhd",
        prob_window.astype(jnp.bfloat16),
        grad_blocks,
        preferred_element_type=jnp.float32,
    )
    key_first = (
        jnp.einsum("hibk,ibhd->khd", dscore_first, query_blocks, preferred_element_type=jnp.float32)
        * softmax_scale
    )
    value_first = jnp.einsum(
        "hibk,ibhd->khd",
        prob_first.astype(jnp.bfloat16),
        grad_blocks,
        preferred_element_type=jnp.float32,
    )
    key_far = (
        jnp.einsum(
            "hibrt,ibhd->irhtd", dscore_far, query_blocks, preferred_element_type=jnp.float32
        )
        * softmax_scale
    )
    value_far = jnp.einsum(
        "hibrt,ibhd->irhtd",
        prob_far.astype(jnp.bfloat16),
        grad_blocks,
        preferred_element_type=jnp.float32,
    )
    window_terms = jnp.stack(
        [
            key_window.reshape(block_count, 3, block_len, head_count, head_dim),
            value_window.reshape(block_count, 3, block_len, head_count, head_dim),
        ],
        axis=3,
    )
    grad_pad = jnp.zeros((block_count + 2, block_len, 2, head_count, head_dim), jnp.float32)
    grad_pad = (
        grad_pad.at[:block_count]
        .add(window_terms[:, 0])
        .at[1 : block_count + 1]
        .add(window_terms[:, 1])
        .at[2:]
        .add(window_terms[:, 2])
    )
    global_grad = lax.psum(jnp.stack([key_first, value_first], axis=1), "seq")
    grad_pad = grad_pad.at[1].add(jnp.where(seq_index == 0, global_grad, 0.0))
    rims = jnp.concatenate([grad_pad[0], grad_pad[block_count + 1]], axis=0).reshape(
        2 * block_len, 2 * width_cols
    )
    rim_sums = with_halo(rims.astype(jnp.bfloat16), (("seq", 0),), block_len).astype(rims.dtype)
    core = grad_pad[1 : block_count + 1].reshape(shard_len, 2 * width_cols)
    core = (
        core.at[:block_len]
        .add(rim_sums[:block_len])
        .at[shard_len - block_len :]
        .add(rim_sums[3 * block_len :])
    )
    core = core.reshape(block_count, block_len, 2, head_count, head_dim)
    far_terms = (
        jnp.stack([key_far, value_far], axis=4)
        .reshape(request_count, block_len, 2, head_dim)
        .astype(jnp.bfloat16)
    )
    outgoing = (
        jnp.zeros((seq_count * capacity, block_len, 2, head_dim), jnp.bfloat16)
        .at[slot_of]
        .set(far_terms)
    )
    outgoing = outgoing.reshape(seq_count, capacity, block_len, 2 * head_dim)
    incoming = (
        lax.all_to_all(outgoing, "seq", split_axis=0, concat_axis=0, tiled=True)
        .reshape(seq_count, capacity, block_len, 2, head_dim)
        .astype(jnp.float32)
    )
    incoming = jnp.where(is_valid[:, :, None, None, None], incoming, 0.0)
    core = core.at[asked_block, :, :, asked_head, :].add(incoming)
    grad_k = core[:, :, 0].reshape(shard_len, width_cols).astype(jnp.bfloat16)
    grad_v = core[:, :, 1].reshape(shard_len, width_cols).astype(jnp.bfloat16)
    grad_q_rows = grad_q.reshape(shard_len, width_cols)
    grad_queries, grad_keys, grad_values = (
        lax.all_to_all(grad_q_rows[None], "head", split_axis=1, concat_axis=2, tiled=True),
        lax.all_to_all(grad_k[None], "head", split_axis=1, concat_axis=2, tiled=True),
        lax.all_to_all(grad_v[None], "head", split_axis=1, concat_axis=2, tiled=True),
    )
    return (layer_out, grad_queries, grad_keys, grad_values, weight_grad)


def solution(mesh):
    in_specs = (
        P("dp", ("seq", "head"), None),
        P("dp", ("seq", "head"), None),
        P("dp", ("seq", "head"), None),
        P("seq", "head", None),
        P("head", None),
        P("dp", ("seq", "head"), None),
    )
    out_specs = (
        P("dp", ("seq", "head"), None),
        P("dp", ("seq", "head"), None),
        P("dp", ("seq", "head"), None),
        P("dp", ("seq", "head"), None),
        P("head", None),
    )
    return jax.shard_map(
        per_device, mesh=mesh, in_specs=in_specs, out_specs=out_specs, check_vma=False
    )
```

profile of v0, /device:TPU:70, one launch (start us, length us, event | category | flops | bytes accessed | tf_op | source)
XLA Modules:
  0.0 795.7 jit_solution(17635221475031465558)
XLA Ops:
  13.4 7.4 all-to-all-start.3
  27.1 12.6 %reduce.16 = bf16[2048,160]{1,0:T(8,128)(2,1)S(1)} reduce(bf16[2048,1,160]{2,1,0:T(2,128)(2,1)} %bitcast.313, bf16[]{:T(256)} %broadcast.542), dimensions={1}, to_apply=%bitcast.270.reduce_sub_computation | reduce | bytes 1310722
  52.4 12.6 %reduce.17 = bf16[2048,160]{1,0:T(8,128)(2,1)S(1)} reduce(bf16[2048,1,160]{2,1,0:T(2,128)(2,1)} %bitcast.317, bf16[]{:T(256)} %broadcast.542), dimensions={1}, to_apply=%bitcast.272.reduce_sub_computation | reduce | bytes 1310722
  78.3 12.6 %reduce.15 = bf16[2048,160]{1,0:T(8,128)(2,1)S(1)} reduce(bf16[2048,1,160]{2,1,0:T(2,128)(2,1)} %bitcast.318, bf16[]{:T(256)} %broadcast.542), dimensions={1}, to_apply=%bitcast.274.reduce_sub_computation | reduce | bytes 1310722
  142.2 12.2 %gather_fusion = bf16[240,64,2,128]{3,1,2,0:T(8,128)(2,1)} fusion(bf16[10,64,2,4,128]{4,1,3,2,0:T(8,128)(2,1)S(1)} %copy.335, s32[240]{0:T(256)S(1)} %reshape.602), kind=kCustom, calls=%fused_computation | custom fusion | bytes 15730560 | tf_op jit(solution)/shard_map/gather | solution.py:69
  154.4 15.3 %copy.336 = bf16[240,64,2,128]{3,2,1,0:T(2,128)(2,1)} copy(bf16[240,64,2,128]{3,1,2,0:T(8,128)(2,1)} %gather_fusion) | data formatting | bytes 15728640 | tf_op jit(solution)/shard_map/gather | solution.py:69
  169.7 13.4 %gather.9 = bf16[16,15,64,256]{3,2,1,0:T(8,128)(2,1)} reshape(bf16[240,64,2,128]{3,2,1,0:T(2,128)(2,1)} %copy.336) | data formatting | bytes 15728640 | tf_op jit(solution)/shard_map/gather | solution.py:69
  183.1 7.0 broadcast_select_fusion.1
  190.1 7.1 all-to-all-start.4
  231.7 108.0 %all-reduce.6.cloned.1.call-done = bf16[64,2,4,128]{3,0,2,1:T(8,128)(2,1)} async-done(((bf16[64,2,4,128]{3,0,2,1:T(8,128)(2,1)}), bf16[64,2,4,128]{3,0,2,1:T(8,128)(2,1)}) %all-reduce.6.cloned.1.call-update) | async-done | bytes 131088 | tf_op jit(solution)/shard_map/psum | solution.py:27
  355.2 12.2 %reshape.589 = bf16[240,64,2,128]{3,2,1,0:T(2,128)(2,1)} reshape(bf16[16,15,64,256]{3,2,1,0:T(8,128)(2,1)} %all-to-all-done.4) | data formatting | bytes 15728640 | tf_op jit(solution)/shard_map/reshape | solution.py:73
  367.4 8.5 %copy.337 = bf16[240,64,2,128]{3,1,2,0:T(8,128)(2,1)} copy(bf16[240,64,2,128]{3,2,1,0:T(2,128)(2,1)} %reshape.589) | data formatting | bytes 15728640 | tf_op jit(solution)/shard_map/reshape | solution.py:73
  375.9 11.2 %gather_fusion.1 = bf16[160,64,2,128]{3,1,2,0:T(8,128)(2,1)} fusion(bf16[240,64,2,128]{3,1,2,0:T(8,128)(2,1)} %copy.337, s32[1024]{0:T(1024)S(1)} %pad_clamp_fusion), kind=kCustom, calls=%fused_computation.1 | custom fusion | bytes 10486400 | tf_op jit(solution)/shard_map/gather | solution.py:73
  387.2 7.3 slice_bitcast_fusion.5
  441.9 24.3 %scatter_fusion = bf16[240,64,2,128]{3,1,2,0:T(8,128)(2,1)} fusion(bf16[240,64,2,128]{3,1,2,0:T(8,128)(2,1)} %broadcast_in_dim.101, s32[160]{0:T(256)S(1)} %bitcast.345, bf16[160,64,2,128]{3,1,2,0:T(8,128)(2,1)} %copy.383), kind=kCustom, calls=%fused_computation.3 | custom fusion | bytes 15729280 | tf_op jit(solution)/shard_map/scatter | solution.py:251
  466.2 15.4 %copy.384 = bf16[240,64,2,128]{3,2,1,0:T(2,128)(2,1)} copy(bf16[240,64,2,128]{3,1,2,0:T(8,128)(2,1)} %scatter_fusion) | data formatting | bytes 15728640 | tf_op jit(solution)/shard_map/scatter | solution.py:251
  481.5 13.4 %reshape.599 = bf16[16,15,64,256]{3,2,1,0:T(8,128)(2,1)} reshape(bf16[240,64,2,128]{3,2,1,0:T(2,128)(2,1)} %copy.384) | data formatting | bytes 15728640 | tf_op jit(solution)/shard_map/reshape | solution.py:253
  494.9 7.4 all-to-all-start.6
  564.8 43.4 %collective-permute-done.3 = bf16[64,1024]{1,0:T(8,128)(2,1)S(1)} collective-permute-done((bf16[64,1024]{1,0:T(8,128)(2,1)S(1)}, bf16[64,1024]{1,0:T(8,128)(2,1)S(1)}, u32[]{:S(2)}, u32[]{:S(2)}) %collective-permute-start.3) | collective-permute-done | bytes 131104 | tf_op jit(solution)/shard_map/ppermute | solution.py:20
  608.2 14.8 %collective-permute-done.2 = bf16[64,1024]{1,0:T(8,128)(2,1)S(1)} collective-permute-done((bf16[64,1024]{1,0:T(8,128)(2,1)S(1)}, bf16[64,1024]{1,0:T(8,128)(2,1)S(1)}, u32[]{:S(2)}, u32[]{:S(2)}) %collective-permute-start.2) | collective-permute-done | bytes 131104 | tf_op jit(solution)/shard_map/ppermute | solution.py:17
  637.9 16.2 %reshape.601 = f32[16,15,64,2,128]{4,3,2,1,0:T(2,128)} reshape(bf16[16,15,64,256]{3,2,1,0:T(8,128)(2,1)} %all-to-all-done.6) | data formatting | bytes 23592960 | tf_op jit(solution)/shard_map/convert_element_type | solution.py:257
  654.1 12.1 %broadcast_select_fusion = f32[16,15,64,2,128]{4,3,2,1,0:T(2,128)} fusion(f32[16,15,64,2,128]{4,3,2,1,0:T(2,128)} %reshape.601, pred[16,15]{1,0:T(8,128)(4,1)S(1)} %compare_bitcast_fusion), kind=kLoop, calls=%fused_computation.5 | loop fusion | flops 3932160 | bytes 31457520 | tf_op jit(solution)/shard_map/jit(_where)/select_n | solution.py:259
  666.2 13.5 %copy.386 = f32[240,64,2,128]{3,1,2,0:T(8,128)} copy(f32[240,64,2,128]{3,2,1,0:T(2,128)} %bitcast.298) | data formatting | bytes 31457280 | tf_op jit(solution)/shard_map/jit(_where)/select_n | solution.py:259
  679.7 50.5 %scatter_fusion.1 = f32[10,64,2,4,128]{4,1,3,2,0:T(8,128)} fusion(f32[10,64,2,4,128]{4,1,3,2,0:T(8,128)} %copy.385, s32[240]{0:T(256)S(1)} %reshape.632, f32[240,64,2,128]{3,1,2,0:T(8,128)} %copy.386), kind=kCustom, calls=%fused_computation.4 | custom fusion | flops 3932160 | bytes 47187840 | tf_op jit(solution)/shard_map/scatter-add | solution.py:260
  (258 shorter events, 321.3 us)
Async XLA Ops:
  8.0 341.4 %copy-start = (bf16[512,2048]{1,0:T(8,128)(2,1)S(1)}, bf16[512,2048]{1,0:T(8,128)(2,1)}, u32[]{:S(2)}) copy-start(bf16[512,2048]{1,0:T(8,128)(2,1)} %param.22) | copy-start | bytes 6291460
  11.6 15.0 %copy-start.31 = (s32[160,1]{0,1:T(1,128)}, s32[160,1]{0,1:T(1,128)S(1)}, u32[]{:S(2)}) copy-start(s32[160,1]{0,1:T(1,128)S(1)} %compare_select_fusion.2) | copy-start | bytes 1924
  13.4 28.6 %all-to-all-start.3 = ((s32[16,1,15]{2,1,0:T(1,128)}), s32[16,1,15]{2,1,0:T(1,128)S(1)}, u32[]{:S(2)}, u32[]{:S(2)}) async-start(s32[16,1,15]{2,1,0:T(1,128)} %bitcast.19), calls=%async_computation.3 | async-start | bytes 16384 | tf_op jit(solution)/shard_map/all_to_all | solution.py:64
  42.1 25.2 %all-to-all-start.1 = ((bf16[4,2,40960]{2,1,0:T(2,128)(2,1)}), bf16[4,2,40960]{2,1,0:T(2,128)(2,1)}, u32[]{:S(2)}, u32[]{:S(2)}) async-start(bf16[4,2,40960]{2,1,0:T(2,128)(2,1)} %reshape.653), calls=%async_computation.1 | async-start | bytes 1310720 | tf_op jit(solution)/shard_map/all_to_all | solution.py:38
  67.3 35.9 %all-to-all-start = ((bf16[4,2,40960]{2,1,0:T(2,128)(2,1)}), bf16[4,2,40960]{2,1,0:T(2,128)(2,1)}, u32[]{:S(2)}, u32[]{:S(2)}) async-start(bf16[4,2,40960]{2,1,0:T(2,128)(2,1)} %reshape.655), calls=%async_computation | async-start | bytes 1310720 | tf_op jit(solution)/shard_map/all_to_all | solution.py:37
  103.2 17.0 %copy-start.20 = (bf16[1,4,160,512]{3,2,1,0:T(8,128)(2,1)}, bf16[1,4,160,512]{3,2,1,0:T(8,128)(2,1)S(1)}, u32[]{:S(2)}) copy-start(bf16[1,4,160,512]{3,2,1,0:T(8,128)(2,1)S(1)} %copy.316) | copy-start | bytes 1966084
  103.2 86.9 %all-to-all-start.2 = ((bf16[4,2,40960]{2,1,0:T(2,128)(2,1)}), bf16[4,2,40960]{2,1,0:T(2,128)(2,1)}, u32[]{:S(2)}, u32[]{:S(2)}) async-start(bf16[4,2,40960]{2,1,0:T(2,128)(2,1)} %reshape.657), calls=%async_computation.2 | async-start | bytes 1310720 | tf_op jit(solution)/shard_map/all_to_all | solution.py:36
  120.2 6.9 collective-permute-start
  123.3 9.0 %collective-permute-start.1 = (bf16[64,1024]{1,0:T(8,128)(2,1)S(1)}, bf16[64,1024]{1,0:T(8,128)(2,1)S(1)}, u32[]{:S(2)}, u32[]{:S(2)}) collective-permute-start(bf16[64,1024]{1,0:T(8,128)(2,1)S(1)} %get-tuple-element.80), channel_id=1, source_target_pairs={{4,0},{8,4},{12,8},{16,12},{20,16},{24,20},{28,24},{32,28},{36,32}... | collective-permute-start | bytes 393224 | tf_op jit(solution)/shard_map/ppermute | solution.py:20
  190.1 9.0 %copy-start.32 = (s32[160,1]{0,1:T(1,128)S(1)}, s32[160,1]{0,1:T(1,128)}, u32[]{:S(2)}) copy-start(s32[160,1]{0,1:T(1,128)} %copy-done.31) | copy-start | bytes 1924
  190.1 165.2 %all-to-all-start.4 = ((bf16[16,15,64,256]{3,2,1,0:T(8,128)(2,1)}), bf16[16,15,64,256]{3,2,1,0:T(8,128)(2,1)}, u32[]{:S(2)}, u32[]{:S(2)}) async-start(bf16[16,15,64,256]{3,2,1,0:T(8,128)(2,1)} %broadcast_select_fusion.1), calls=%async_computation.4 | async-start | bytes 15728640 | tf_op jit(solution)/shard_map/all_to_all | solution.py:72
  197.1 142.6 %all-reduce.6.cloned.1.call-start = ((), (), s32[]{:S(2)}) async-start(), calls=%async_computation.10 | async-start | bytes 262144 | tf_op jit(solution)/shard_map/psum | solution.py:27
  198.0 151.5 %all-gather.2.cloned.1.call-start = ((), (), s32[]{:S(2)}) async-start(), calls=%async_computation.12 | async-start | bytes 3276800 | tf_op jit(solution)/shard_map/all_gather | solution.py:144
  198.5 330.6 %all-reduce.8.cloned.1.call-start = ((), (), s32[]{:S(2)}) async-start(), calls=%async_computation.13 | async-start | bytes 524288 | tf_op jit(solution)/shard_map/psum | solution.py:229
  228.7 111.1 %copy-start.10 = (bf16[10,64,4,128]{3,2,1,0:T(4,128)(2,1)S(1)}, bf16[10,64,4,128]{3,2,1,0:T(4,128)(2,1)}, u32[]{:S(2)}) copy-start(bf16[10,64,4,128]{3,2,1,0:T(4,128)(2,1)} %reshape_squeeze.2) | copy-start | bytes 1966084
  355.2 59.4 %copy-start.2 = (bf16[10,64,4,128]{3,2,1,0:T(4,128)(2,1)}, bf16[10,64,4,128]{3,2,1,0:T(4,128)(2,1)S(1)}, u32[]{:S(2)}) copy-start(bf16[10,64,4,128]{3,2,1,0:T(4,128)(2,1)S(1)} %reshape.592) | copy-start | bytes 1966084
  412.3 361.5 %all-reduce.10.cloned.1.call-start = ((), (), s32[]{:S(2)}) async-start(), calls=%async_computation.14 | async-start | bytes 8388608 | tf_op jit(solution)/shard_map/psum | solution.py:150
  494.9 138.3 %all-to-all-start.6 = ((bf16[16,15,64,256]{3,2,1,0:T(8,128)(2,1)}), bf16[16,15,64,256]{3,2,1,0:T(8,128)(2,1)}, u32[]{:S(2)}, u32[]{:S(2)}) async-start(bf16[16,15,64,256]{3,2,1,0:T(8,128)(2,1)} %reshape.599), calls=%async_computation.7 | async-start | bytes 15728640 | tf_op jit(solution)/shard_map/all_to_all | solution.py:255
  502.3 283.8 %reduce-scatter.2.cloned.1.call-start = ((), (), s32[]{:S(2)}) async-start(), calls=%async_computation.11 | async-start | bytes 6553600 | tf_op jit(solution)/shard_map/reduce_scatter | solution.py:138
  533.4 74.8 %collective-permute-start.3 = (bf16[64,1024]{1,0:T(8,128)(2,1)S(1)}, bf16[64,1024]{1,0:T(8,128)(2,1)S(1)}, u32[]{:S(2)}, u32[]{:S(2)}) collective-permute-start(bf16[64,1024]{1,0:T(8,128)(2,1)S(1)} %concatenate.44), channel_id=1, source_target_pairs={{4,0},{8,4},{12,8},{16,12},{20,16},{24,20},{28,24},{32,28},{36,32}... | collective-permute-start | bytes 393224 | tf_op jit(solution)/shard_map/ppermute | solution.py:20
  536.4 86.6 %collective-permute-start.2 = (bf16[64,1024]{1,0:T(8,128)(2,1)S(1)}, bf16[64,1024]{1,0:T(8,128)(2,1)S(1)}, u32[]{:S(2)}, u32[]{:S(2)}) collective-permute-start(bf16[64,1024]{1,0:T(8,128)(2,1)S(1)} %concatenate.43), channel_id=1, source_target_pairs={{0,4},{4,8},{8,12},{12,16},{16,20},{20,24},{24,28},{28,32},{32,36}... | collective-permute-start | bytes 393224 | tf_op jit(solution)/shard_map/ppermute | solution.py:17
  633.3 113.3 %all-to-all-start.5 = ((bf16[4,2,40960]{2,1,0:T(2,128)(2,1)}), bf16[4,2,40960]{2,1,0:T(2,128)(2,1)}, u32[]{:S(2)}, u32[]{:S(2)}) async-start(bf16[4,2,40960]{2,1,0:T(2,128)(2,1)} %reshape.659), calls=%async_computation.6 | async-start | bytes 1310720 | tf_op jit(solution)/shard_map/all_to_all | solution.py:265
  746.5 22.5 %all-to-all-start.7 = ((bf16[4,2,40960]{2,1,0:T(2,128)(2,1)}), bf16[4,2,40960]{2,1,0:T(2,128)(2,1)}, u32[]{:S(2)}, u32[]{:S(2)}) async-start(bf16[4,2,40960]{2,1,0:T(2,128)(2,1)} %reshape.661), calls=%async_computation.8 | async-start | bytes 1310720 | tf_op jit(solution)/shard_map/all_to_all | solution.py:266
  769.0 13.7 %all-to-all-start.8 = ((bf16[4,2,40960]{2,1,0:T(2,128)(2,1)}), bf16[4,2,40960]{2,1,0:T(2,128)(2,1)}, u32[]{:S(2)}, u32[]{:S(2)}) async-start(bf16[4,2,40960]{2,1,0:T(2,128)(2,1)} %reshape.663), calls=%async_computation.9 | async-start | bytes 1310720 | tf_op jit(solution)/shard_map/all_to_all | solution.py:267
  (29 other events, 86.0 us)
Sparse Core Ops, SparseCore 0:
  201.7 137.9 all-reduce.5
  412.4 84.3 all-reduce.7
  500.8 193.4 all-reduce.9
Sparse Core Ops, SparseCore 1:
  200.1 36.8 all-gather.1
  506.3 56.6 reduce-scatter.1
where the time goes:
time: 808 us; the launch traced here: 796 us
  local copies, waits for them, and re-layouts  324 us (40%)
  other arithmetic  173 us (21%)
  waiting for transfers between devices  173 us (21%)
  starting transfers between devices  65.9 us (8%)
  matrix products  43.6 us (5%)
  between operations  16.2 us (2%)
    psum x1, waiting for transfers between devices, from_root(): return lax.psum(block, axis)  108 us
    unnamed x90, local copies, waits for them, and re-layouts  62.3 us
    unnamed x7, other arithmetic  53.9 us
    scatter-add x1, other arithmetic, per_device(): core = core.at[asked_block, :, :, asked_head, :].add(incoming)  50.5 us
    ppermute x2, waiting for transfers between devices, with_halo(): lax.ppermute(lax.slice_in_dim(block, 0, width, axis=dim), axis, backward)  48.6 us
    gather x3, local copies, waits for them, and re-layouts, per_device(): served = block_view[asked_block, :, :, asked_head, :]  40.9 us
    scatter x2, local copies, waits for them, and re-layouts, per_device(): outgoing = jnp.zeros((seq_count * capacity, block_len, 2, head_dim), jnp....  39.6 us
    reshape x2, local copies, waits for them, and re-layouts, per_device(): received.reshape(seq_count * capacity, block_len, 2, head_dim)[slot_of]  20.7 us
  transfers between devices with their start and end apart: 18, of which 6 were waited for; matrix products, arithmetic and copies ran while one was open for 58% of the time, Pallas kernels for 0%

commit v1 on v0

--- a/solution.py
+++ b/solution.py
@@ -22,9 +22,28 @@
     return block
 
 
-def from_root(block, axis, holder):
-    block = jnp.where(lax.axis_index(axis) == holder, block, jnp.zeros_like(block))
-    return lax.psum(block, axis)
+def broadcast_first(block, axis):
+    count = lax.axis_size(axis)
+    index = lax.axis_index(axis)
+    step = 1
+    while step < count:
+        pairs = [(i, i + step) for i in range(step) if i + step < count]
+        got = lax.ppermute(block, axis, pairs)
+        block = jnp.where(index >= step, got, block)
+        step *= 2
+    return block
+
+
+def reduce_to_first(block, axis):
+    count = lax.axis_size(axis)
+    step = 1
+    while step * 2 < count:
+        step *= 2
+    while step >= 1:
+        pairs = [(i + step, i) for i in range(step) if i + step < count]
+        block = block + lax.ppermute(block, axis, pairs)
+        step //= 2
+    return block
 
 
 def per_device(queries, key_rows, values, rand_blocks, out_weight, cotangent):
@@ -45,7 +64,7 @@
     rand_count = rand_blocks.shape[2]
     key_value = jnp.concatenate([k_heads[0], v_heads[0]], axis=1)
     padded = with_halo(key_value, (("seq", 0),), block_len)
-    first_block = from_root(key_value[:block_len], "seq", 0)
+    first_block = broadcast_first(key_value[:block_len], "seq")
     requests = jnp.transpose(rand_blocks, (0, 2, 1)).reshape(-1)
     request_count = requests.shape[0]
     head_of = jnp.arange(request_count, dtype=jnp.int32) % head_count
@@ -62,15 +81,24 @@
         .reshape(seq_count, capacity)
     )
     asked_here = lax.all_to_all(asked_codes, "seq", split_axis=0, concat_axis=0, tiled=True)
-    is_valid = asked_here >= 0
-    asked_block = jnp.maximum(asked_here, 0) // head_count
-    asked_head = jnp.maximum(asked_here, 0) % head_count
-    block_view = key_value.reshape(block_count, block_len, 2, head_count, head_dim)
-    served = block_view[asked_block, :, :, asked_head, :]
-    served = jnp.where(is_valid[:, :, None, None, None], served, jnp.zeros_like(served))
+    slot_total = seq_count * capacity
+    pair_count = block_count * head_count
+    asked_flat = asked_here.reshape(slot_total)
+    serve_hot = (
+        asked_flat[:, None] == jnp.arange(pair_count, dtype=jnp.int32)[None, :]
+    ).astype(jnp.bfloat16)
+    pick_hot = (
+        slot_of[:, None] == jnp.arange(slot_total, dtype=jnp.int32)[None, :]
+    ).astype(jnp.bfloat16)
+    kv_pairs = jnp.transpose(
+        key_value.reshape(block_count, block_len, 2, head_count, head_dim), (0, 3, 1, 2, 4)
+    ).reshape(pair_count, block_len * 2 * head_dim)
+    served = jnp.dot(serve_hot, kv_pairs, preferred_element_type=jnp.float32).astype(jnp.bfloat16)
     served = served.reshape(seq_count, capacity, block_len, 2 * head_dim)
     received = lax.all_to_all(served, "seq", split_axis=0, concat_axis=0, tiled=True)
-    far_pairs = received.reshape(seq_count * capacity, block_len, 2, head_dim)[slot_of]
+    far_pairs = jnp.dot(
+        pick_hot, received.reshape(slot_total, -1), preferred_element_type=jnp.float32
+    ).astype(jnp.bfloat16)
     pair_view = padded.reshape(block_count + 2, block_len, 2, head_count, head_dim)
     window_pairs = jnp.stack(
         [pair_view[:block_count], pair_view[1 : block_count + 1], pair_view[2:]], axis=1
@@ -80,9 +108,9 @@
     first_pairs = first_block.reshape(block_len, 2, head_count, head_dim)
     first_keys = first_pairs[:, 0]
     first_vals = first_pairs[:, 1]
-    far_view = far_pairs.reshape(block_count, rand_count, head_count, block_len, 2, head_dim)
-    far_keys = far_view[:, :, :, :, 0]
-    far_vals = far_view[:, :, :, :, 1]
+    far_view = far_pairs.reshape(block_count, rand_count, head_count, block_len, 2 * head_dim)
+    far_keys = far_view[..., :head_dim]
+    far_vals = far_view[..., head_dim:]
     global_ids = seq_index * block_count + jnp.arange(block_count, dtype=jnp.int32)
     block_total = seq_count * block_count
     window_live = jnp.stack([global_ids > 0, global_ids >= 0, global_ids < block_total - 1], axis=1)
@@ -226,7 +254,9 @@
         .at[2:]
         .add(window_terms[:, 2])
     )
-    global_grad = lax.psum(jnp.stack([key_first, value_first], axis=1), "seq")
+    global_grad = reduce_to_first(
+        jnp.stack([key_first, value_first], axis=1).reshape(block_len, 2 * width_cols), "seq"
+    ).reshape(block_len, 2, head_count, head_dim)
     grad_pad = grad_pad.at[1].add(jnp.where(seq_index == 0, global_grad, 0.0))
     rims = jnp.concatenate([grad_pad[0], grad_pad[block_count + 1]], axis=0).reshape(
         2 * block_len, 2 * width_cols
@@ -241,23 +271,19 @@
     )
     core = core.reshape(block_count, block_len, 2, head_count, head_dim)
     far_terms = (
-        jnp.stack([key_far, value_far], axis=4)
-        .reshape(request_count, block_len, 2, head_dim)
+        jnp.concatenate([key_far, value_far], axis=-1)
+        .reshape(request_count, block_len * 2 * head_dim)
         .astype(jnp.bfloat16)
     )
-    outgoing = (
-        jnp.zeros((seq_count * capacity, block_len, 2, head_dim), jnp.bfloat16)
-        .at[slot_of]
-        .set(far_terms)
+    outgoing = jnp.dot(pick_hot.T, far_terms, preferred_element_type=jnp.float32).astype(
+        jnp.bfloat16
     )
     outgoing = outgoing.reshape(seq_count, capacity, block_len, 2 * head_dim)
-    incoming = (
-        lax.all_to_all(outgoing, "seq", split_axis=0, concat_axis=0, tiled=True)
-        .reshape(seq_count, capacity, block_len, 2, head_dim)
-        .astype(jnp.float32)
-    )
-    incoming = jnp.where(is_valid[:, :, None, None, None], incoming, 0.0)
-    core = core.at[asked_block, :, :, asked_head, :].add(incoming)
+    incoming = lax.all_to_all(outgoing, "seq", split_axis=0, concat_axis=0, tiled=True)
+    added = jnp.dot(
+        serve_hot.T, incoming.reshape(slot_total, -1), preferred_element_type=jnp.float32
+    ).reshape(block_count, head_count, block_len, 2, head_dim)
+    core = core + jnp.transpose(added, (0, 2, 3, 1, 4))
     grad_k = core[:, :, 0].reshape(shard_len, width_cols).astype(jnp.bfloat16)
     grad_v = core[:, :, 1].reshape(shard_len, width_cols).astype(jnp.bfloat16)
     grad_q_rows = grad_q.reshape(shard_len, width_cols)

time: 808 us -> 657 us (0.81)
  the two profiles are of different devices: /device:TPU:70 before, /device:TPU:0 now
where the time goes in v1:
time: 657 us; the launch traced here: 645 us
  local copies, waits for them, and re-layouts  209 us (32%)
  waiting for transfers between devices  175 us (27%)
  other arithmetic  95.2 us (14%)
  starting transfers between devices  80.8 us (12%)
  matrix products  69.2 us (11%)
  between operations  15.3 us (2%)
    unnamed x92, local copies, waits for them, and re-layouts  111 us
    ppermute x4, waiting for transfers between devices, reduce_to_first(): block = block + lax.ppermute(block, axis, pairs)  95.5 us
    ppermute x4, waiting for transfers between devices, broadcast_first(): got = lax.ppermute(block, axis, pairs)  78.6 us
    unnamed x6, other arithmetic  51.8 us
    dot_general x1, local copies, waits for them, and re-layouts, per_device(): jnp.dot(serve_hot.T, incoming.reshape(slot_total, -1), preferred_element_...  13.9 us
  transfers between devices with their start and end apart: 24, of which 7 were waited for; matrix products, arithmetic and copies ran while one was open for 44% of the time, Pallas kernels for 0%

profile of v1, /device:TPU:0, one launch (start us, length us, event | category | flops | bytes accessed | tf_op | source)
XLA Modules:
  0.0 644.7 jit_solution(16865927430126323125)
XLA Ops:
  7.2 6.0 copy.227
  13.7 12.7 %reduce.20 = bf16[2048,160]{1,0:T(8,128)(2,1)S(1)} reduce(bf16[2048,1,160]{2,1,0:T(2,128)(2,1)} %bitcast.285, bf16[]{:T(256)} %broadcast.366), dimensions={1}, to_apply=%bitcast.240.reduce_sub_computation | reduce | bytes 1310722
  34.1 5.9 copy.230
  39.9 12.6 %reduce.21 = bf16[2048,160]{1,0:T(8,128)(2,1)S(1)} reduce(bf16[2048,1,160]{2,1,0:T(2,128)(2,1)} %bitcast.289, bf16[]{:T(256)} %broadcast.366), dimensions={1}, to_apply=%bitcast.238.reduce_sub_computation | reduce | bytes 1310722
  74.8 5.7 copy.231
  90.1 9.4 %all-to-all-start.3 = ((s32[16,1,15]{2,1,0:T(1,128)}), s32[16,1,15]{2,1,0:T(1,128)S(1)}, u32[]{:S(2)}, u32[]{:S(2)}) async-start(s32[16,1,15]{2,1,0:T(1,128)} %bitcast.19), calls=%async_computation.3 | async-start | bytes 16384 | tf_op jit(solution)/shard_map/all_to_all | solution.py:83
  99.5 5.9 copy.235
  105.4 12.6 %reduce.19 = bf16[2048,160]{1,0:T(8,128)(2,1)S(1)} reduce(bf16[2048,1,160]{2,1,0:T(2,128)(2,1)} %bitcast.290, bf16[]{:T(256)} %broadcast.366), dimensions={1}, to_apply=%bitcast.242.reduce_sub_computation | reduce | bytes 1310722
  141.6 6.7 %convolution_convert_fusion.1 = bf16[240,16384]{1,0:T(8,128)(2,1)} fusion(bf16[40,16384]{1,0:T(8,128)(2,1)} %reshape.545, s32[240]{0:T(256)S(1)} %eq.85), kind=kOutput, calls=%fused_computation.2 | convolution fusion | flops 318514560 | bytes 9176000 | tf_op jit(solution)/shard_map/dot_general | solution.py:96
  148.2 8.7 %copy.340 = bf16[30,8,64,256]{3,2,1,0:T(8,128)(2,1)} copy(bf16[30,8,64,256]{3,1,2,0:T(8,128)(2,1)} %bitcast.266) | data formatting | bytes 15728640
  156.9 7.3 %all-to-all-start.4 = ((bf16[16,15,64,256]{3,2,1,0:T(8,128)(2,1)}), bf16[16,15,64,256]{3,2,1,0:T(8,128)(2,1)}, u32[]{:S(2)}, u32[]{:S(2)}) async-start(bf16[16,15,64,256]{3,2,1,0:T(8,128)(2,1)} %bitcast.269), calls=%async_computation.4 | async-start | bytes 15728640 | tf_op jit(solution)/shard_map/all_to_all | solution.py:98
  175.1 5.7 copy.236
  189.7 78.3 %collective-permute-done.2 = bf16[64,1024]{1,0:T(8,128)(2,1)} collective-permute-done((bf16[64,1024]{1,0:T(8,128)(2,1)S(1)}, bf16[64,1024]{1,0:T(8,128)(2,1)}, u32[]{:S(2)}, u32[]{:S(2)}) %collective-permute-start.2) | collective-permute-done | bytes 131104 | tf_op jit(solution)/shard_map/ppermute | solution.py:31
  299.3 14.4 %copy.341 = bf16[30,8,64,256]{3,1,2,0:T(8,128)(2,1)} copy(bf16[30,8,64,256]{3,2,1,0:T(8,128)(2,1)} %bitcast.108) | data formatting | bytes 15728640
  366.6 5.6 convolution_convert_fusion
  372.2 8.9 %copy.345 = bf16[30,8,64,256]{3,2,1,0:T(8,128)(2,1)} copy(bf16[30,8,64,256]{3,1,2,0:T(8,128)(2,1)} %bitcast.265) | data formatting | bytes 15728640
  381.1 9.6 %all-to-all-start.6 = ((bf16[16,15,64,256]{3,2,1,0:T(8,128)(2,1)}), bf16[16,15,64,256]{3,2,1,0:T(8,128)(2,1)}, u32[]{:S(2)}, u32[]{:S(2)}) async-start(bf16[16,15,64,256]{3,2,1,0:T(8,128)(2,1)} %bitcast.268), calls=%async_computation.7 | async-start | bytes 15728640 | tf_op jit(solution)/shard_map/all_to_all | solution.py:282
  411.1 60.6 %collective-permute-done.6 = f32[64,1024]{1,0:T(8,128)S(1)} collective-permute-done((f32[64,1024]{1,0:T(8,128)}, f32[64,1024]{1,0:T(8,128)S(1)}, u32[]{:S(2)}, u32[]{:S(2)}) %collective-permute-start.6) | collective-permute-done | bytes 262176 | tf_op jit(solution)/shard_map/ppermute | solution.py:44
  475.6 13.3 %collective-permute-done.7 = f32[64,1024]{1,0:T(8,128)S(1)} collective-permute-done((f32[64,1024]{1,0:T(8,128)S(1)}, f32[64,1024]{1,0:T(8,128)S(1)}, u32[]{:S(2)}, u32[]{:S(2)}) %collective-permute-start.7) | collective-permute-done | bytes 262176 | tf_op jit(solution)/shard_map/ppermute | solution.py:44
  492.4 13.0 %collective-permute-done.8 = f32[64,1024]{1,0:T(8,128)S(1)} collective-permute-done((f32[64,1024]{1,0:T(8,128)S(1)}, f32[64,1024]{1,0:T(8,128)S(1)}, u32[]{:S(2)}, u32[]{:S(2)}) %collective-permute-start.8) | collective-permute-done | bytes 262176 | tf_op jit(solution)/shard_map/ppermute | solution.py:44
  508.1 8.7 %collective-permute-done.9 = f32[64,1024]{1,0:T(8,128)S(1)} collective-permute-done((f32[64,1024]{1,0:T(8,128)S(1)}, f32[64,1024]{1,0:T(8,128)S(1)}, u32[]{:S(2)}, u32[]{:S(2)}) %collective-permute-start.9) | collective-permute-done | bytes 262176 | tf_op jit(solution)/shard_map/ppermute | solution.py:44
  559.2 14.5 %copy.346 = bf16[30,8,64,256]{3,1,2,0:T(8,128)(2,1)} copy(bf16[30,8,64,256]{3,2,1,0:T(8,128)(2,1)} %bitcast.123) | data formatting | bytes 15728640
  573.7 13.9 %dot_general.103 = bf16[64,2,128,240]{2,1,0,3:T(2,128)(2,1)} reshape(bf16[16384,240]{0,1:T(8,128)(2,1)} %bitcast.270) | data formatting | bytes 15728640 | tf_op jit(solution)/shard_map/dot_general | solution.py:283
  587.6 10.2 %fusion.8 = bf16[10,64,2,4,128]{4,0,2,1,3:T(8,128)(2,1)S(1)} fusion(f32[10,64,2,4,128]{4,3,2,1,0:T(4,128)} %reshape.556, bf16[64,2,128,240]{2,1,0,3:T(2,128)(2,1)} %dot_general.103, s32[10,4]{0,1:T(4,128)S(1)} %multiply_add_fusion, s32[240]{0:T(256)S(1)} %eq.85), kind=kOutput, calls=%fused_computation.19 | convolution fusion | flops 315893120 | bytes 11797600 | tf_op jit(solution)/shard_map/dot_general | solution.py:283
  (264 shorter events, 279.3 us)
Async XLA Ops:
  28.7 26.2 %all-to-all-start = ((bf16[4,2,40960]{2,1,0:T(2,128)(2,1)}), bf16[4,2,40960]{2,1,0:T(2,128)(2,1)}, u32[]{:S(2)}, u32[]{:S(2)}) async-start(bf16[4,2,40960]{2,1,0:T(2,128)(2,1)} %reshape.595), calls=%async_computation | async-start | bytes 1310720 | tf_op jit(solution)/shard_map/all_to_all | solution.py:56
  55.0 15.4 %all-to-all-start.1 = ((bf16[4,2,40960]{2,1,0:T(2,128)(2,1)}), bf16[4,2,40960]{2,1,0:T(2,128)(2,1)}, u32[]{:S(2)}, u32[]{:S(2)}) async-start(bf16[4,2,40960]{2,1,0:T(2,128)(2,1)} %reshape.593), calls=%async_computation.1 | async-start | bytes 1310720 | tf_op jit(solution)/shard_map/all_to_all | solution.py:57
  83.6 42.9 %collective-permute-start = (bf16[64,1024]{1,0:T(8,128)(2,1)S(1)}, bf16[64,1024]{1,0:T(8,128)(2,1)S(1)}, u32[]{:S(2)}, u32[]{:S(2)}) collective-permute-start(bf16[64,1024]{1,0:T(8,128)(2,1)S(1)} %get-tuple-element.96), channel_id=1, source_target_pairs={{0,4},{4,8},{8,12},{12,16},{16,20},{20,24},{24,28},{28,32},{32,36}... | collective-permute-start | bytes 393224 | tf_op jit(solution)/shard_map/ppermute | solution.py:17
  87.0 40.1 %collective-permute-start.1 = (bf16[64,1024]{1,0:T(8,128)(2,1)S(1)}, bf16[64,1024]{1,0:T(8,128)(2,1)}, u32[]{:S(2)}, u32[]{:S(2)}) collective-permute-start(bf16[64,1024]{1,0:T(8,128)(2,1)S(1)} %get-tuple-element.97), channel_id=1, source_target_pairs={{4,0},{8,4},{12,8},{16,12},{20,16},{24,20},{28,24},{32,28},{36,32}... | collective-permute-start | bytes 393224 | tf_op jit(solution)/shard_map/ppermute | solution.py:20
  90.1 30.3 %all-to-all-start.3 = ((s32[16,1,15]{2,1,0:T(1,128)}), s32[16,1,15]{2,1,0:T(1,128)S(1)}, u32[]{:S(2)}, u32[]{:S(2)}) async-start(s32[16,1,15]{2,1,0:T(1,128)} %bitcast.19), calls=%async_computation.3 | async-start | bytes 16384 | tf_op jit(solution)/shard_map/all_to_all | solution.py:83
  120.4 36.6 %all-to-all-start.2 = ((bf16[4,2,40960]{2,1,0:T(2,128)(2,1)}), bf16[4,2,40960]{2,1,0:T(2,128)(2,1)}, u32[]{:S(2)}, u32[]{:S(2)}) async-start(bf16[4,2,40960]{2,1,0:T(2,128)(2,1)} %reshape.597), calls=%async_computation.2 | async-start | bytes 1310720 | tf_op jit(solution)/shard_map/all_to_all | solution.py:55
  156.9 142.3 %all-to-all-start.4 = ((bf16[16,15,64,256]{3,2,1,0:T(8,128)(2,1)}), bf16[16,15,64,256]{3,2,1,0:T(8,128)(2,1)}, u32[]{:S(2)}, u32[]{:S(2)}) async-start(bf16[16,15,64,256]{3,2,1,0:T(8,128)(2,1)} %bitcast.269), calls=%async_computation.4 | async-start | bytes 15728640 | tf_op jit(solution)/shard_map/all_to_all | solution.py:98
  164.2 129.1 %all-gather.2.cloned.1.call-start = ((), (), s32[]{:S(2)}) async-start(), calls=%async_computation.11 | async-start | bytes 3276800 | tf_op jit(solution)/shard_map/all_gather | solution.py:172
  164.9 460.0 %all-reduce.4.cloned.1.call-start = ((), (), s32[]{:S(2)}) async-start(), calls=%async_computation.12 | async-start | bytes 8388608 | tf_op jit(solution)/shard_map/psum | solution.py:178
  165.7 102.3 %collective-permute-start.2 = (bf16[64,1024]{1,0:T(8,128)(2,1)S(1)}, bf16[64,1024]{1,0:T(8,128)(2,1)}, u32[]{:S(2)}, u32[]{:S(2)}) collective-permute-start(bf16[64,1024]{1,0:T(8,128)(2,1)S(1)} %get-tuple-element.97), channel_id=1, source_target_pairs={{0,4},{1,5},{2,6},{3,7},{64,68},{65,69},{66,70},{67,71}} | collective-permute-start | bytes 393224 | tf_op jit(solution)/shard_map/ppermute | solution.py:31
  268.7 12.8 %collective-permute-start.3 = (bf16[64,1024]{1,0:T(8,128)(2,1)}, bf16[64,1024]{1,0:T(8,128)(2,1)S(1)}, u32[]{:S(2)}, u32[]{:S(2)}) collective-permute-start(bf16[64,1024]{1,0:T(8,128)(2,1)} %broadcast_select_fusion), channel_id=1, source_target_pairs={{0,8},{4,12},{1,9},{5,13},{2,10},{6,14},{3,11},{7,15},{64,72},{68,... | collective-permute-start | bytes 393224 | tf_op jit(solution)/shard_map/ppermute | solution.py:31
  282.7 3.8 collective-permute-start.4
  286.5 4.2 collective-permute-start.5
  342.2 293.3 %reduce-scatter.2.cloned.1.call-start = ((), (), s32[]{:S(2)}) async-start(), calls=%async_computation.10 | async-start | bytes 6553600 | tf_op jit(solution)/shard_map/reduce_scatter | solution.py:166
  381.1 173.8 %all-to-all-start.6 = ((bf16[16,15,64,256]{3,2,1,0:T(8,128)(2,1)}), bf16[16,15,64,256]{3,2,1,0:T(8,128)(2,1)}, u32[]{:S(2)}, u32[]{:S(2)}) async-start(bf16[16,15,64,256]{3,2,1,0:T(8,128)(2,1)} %bitcast.268), calls=%async_computation.7 | async-start | bytes 15728640 | tf_op jit(solution)/shard_map/all_to_all | solution.py:282
  393.2 78.5 %collective-permute-start.6 = (f32[64,1024]{1,0:T(8,128)}, f32[64,1024]{1,0:T(8,128)S(1)}, u32[]{:S(2)}, u32[]{:S(2)}) collective-permute-start(f32[64,1024]{1,0:T(8,128)} %reshape.553), channel_id=1, source_target_pairs={{32,0},{36,4},{40,8},{44,12},{48,16},{52,20},{56,24},{60,28},{33,1... | collective-permute-start | bytes 786440 | tf_op jit(solution)/shard_map/ppermute | solution.py:44
  472.7 16.2 %collective-permute-start.7 = (f32[64,1024]{1,0:T(8,128)S(1)}, f32[64,1024]{1,0:T(8,128)S(1)}, u32[]{:S(2)}, u32[]{:S(2)}) collective-permute-start(f32[64,1024]{1,0:T(8,128)S(1)} %add.228), channel_id=1, source_target_pairs={{16,0},{20,4},{24,8},{28,12},{17,1},{21,5},{25,9},{29,13},{18,2},{... | collective-permute-start | bytes 786440 | tf_op jit(solution)/shard_map/ppermute | solution.py:44
  488.9 16.4 %collective-permute-start.8 = (f32[64,1024]{1,0:T(8,128)S(1)}, f32[64,1024]{1,0:T(8,128)S(1)}, u32[]{:S(2)}, u32[]{:S(2)}) collective-permute-start(f32[64,1024]{1,0:T(8,128)S(1)} %add.229), channel_id=1, source_target_pairs={{8,0},{12,4},{9,1},{13,5},{10,2},{14,6},{11,3},{15,7},{72,64},{76,... | collective-permute-start | bytes 786440 | tf_op jit(solution)/shard_map/ppermute | solution.py:44
  505.4 11.4 %collective-permute-start.9 = (f32[64,1024]{1,0:T(8,128)S(1)}, f32[64,1024]{1,0:T(8,128)S(1)}, u32[]{:S(2)}, u32[]{:S(2)}) collective-permute-start(f32[64,1024]{1,0:T(8,128)S(1)} %add.230), channel_id=1, source_target_pairs={{4,0},{5,1},{6,2},{7,3},{68,64},{69,65},{70,66},{71,67}} | collective-permute-start | bytes 786440 | tf_op jit(solution)/shard_map/ppermute | solution.py:44
  523.3 24.0 %collective-permute-start.11 = (bf16[64,1024]{1,0:T(8,128)(2,1)S(1)}, bf16[64,1024]{1,0:T(8,128)(2,1)}, u32[]{:S(2)}, u32[]{:S(2)}) collective-permute-start(bf16[64,1024]{1,0:T(8,128)(2,1)S(1)} %concatenate.41), channel_id=1, source_target_pairs={{4,0},{8,4},{12,8},{16,12},{20,16},{24,20},{28,24},{32,28},{36,32}... | collective-permute-start | bytes 393224 | tf_op jit(solution)/shard_map/ppermute | solution.py:20
  524.6 22.7 %collective-permute-start.10 = (bf16[64,1024]{1,0:T(8,128)(2,1)S(1)}, bf16[64,1024]{1,0:T(8,128)(2,1)}, u32[]{:S(2)}, u32[]{:S(2)}) collective-permute-start(bf16[64,1024]{1,0:T(8,128)(2,1)S(1)} %concatenate.40), channel_id=1, source_target_pairs={{0,4},{4,8},{8,12},{12,16},{16,20},{20,24},{24,28},{28,32},{32,36}... | collective-permute-start | bytes 393224 | tf_op jit(solution)/shard_map/ppermute | solution.py:17
  554.9 50.1 %all-to-all-start.5 = ((bf16[4,2,40960]{2,1,0:T(2,128)(2,1)}), bf16[4,2,40960]{2,1,0:T(2,128)(2,1)}, u32[]{:S(2)}, u32[]{:S(2)}) async-start(bf16[4,2,40960]{2,1,0:T(2,128)(2,1)} %reshape.599), calls=%async_computation.6 | async-start | bytes 1310720 | tf_op jit(solution)/shard_map/all_to_all | solution.py:291
  605.0 15.2 %all-to-all-start.8 = ((bf16[4,2,40960]{2,1,0:T(2,128)(2,1)}), bf16[4,2,40960]{2,1,0:T(2,128)(2,1)}, u32[]{:S(2)}, u32[]{:S(2)}) async-start(bf16[4,2,40960]{2,1,0:T(2,128)(2,1)} %reshape.603), calls=%async_computation.9 | async-start | bytes 1310720 | tf_op jit(solution)/shard_map/all_to_all | solution.py:293
  620.1 13.6 %all-to-all-start.7 = ((bf16[4,2,40960]{2,1,0:T(2,128)(2,1)}), bf16[4,2,40960]{2,1,0:T(2,128)(2,1)S(1)}, u32[]{:S(2)}, u32[]{:S(2)}) async-start(bf16[4,2,40960]{2,1,0:T(2,128)(2,1)} %reshape.601), calls=%async_computation.8 | async-start | bytes 1310720 | tf_op jit(solution)/shard_map/all_to_all | solution.py:292
  (33 other events, 595.9 us)
Sparse Core Ops, SparseCore 0:
  166.7 37.1 all-gather.1
  342.3 194.1 all-reduce.3
  538.9 61.0 reduce-scatter.1

commit v2 on v1

--- a/solution.py
+++ b/solution.py
@@ -51,18 +51,19 @@
     head_dim = HEAD_SIZE
     seq_count = lax.axis_size("seq")
     seq_index = lax.axis_index("seq")
-    q_heads, k_heads, v_heads = (
-        lax.all_to_all(queries, "head", split_axis=2, concat_axis=1, tiled=True),
-        lax.all_to_all(key_rows, "head", split_axis=2, concat_axis=1, tiled=True),
-        lax.all_to_all(values, "head", split_axis=2, concat_axis=1, tiled=True),
-    )
-    q_rows = q_heads[0]
+    group_count = lax.axis_size("head")
+    piece_len = queries.shape[1]
+    width_cols = queries.shape[2] // group_count
+    stacked = jnp.concatenate([queries, key_rows, values], axis=0)
+    stacked = jnp.transpose(stacked.reshape(3, piece_len, group_count, width_cols), (2, 0, 1, 3))
+    stacked = lax.all_to_all(stacked, "head", split_axis=0, concat_axis=0, tiled=True)
+    stacked = jnp.transpose(stacked, (1, 0, 2, 3)).reshape(3, group_count * piece_len, width_cols)
+    q_rows = stacked[0]
     shard_len = q_rows.shape[0]
-    width_cols = q_rows.shape[1]
     head_count = width_cols // head_dim
     block_count = shard_len // block_len
     rand_count = rand_blocks.shape[2]
-    key_value = jnp.concatenate([k_heads[0], v_heads[0]], axis=1)
+    key_value = jnp.concatenate([stacked[1], stacked[2]], axis=1)
     padded = with_halo(key_value, (("seq", 0),), block_len)
     first_block = broadcast_first(key_value[:block_len], "seq")
     requests = jnp.transpose(rand_blocks, (0, 2, 1)).reshape(-1)
@@ -175,7 +176,18 @@
     )
     weight_acc = jnp.dot(attn_rows.T, piece_flat, preferred_element_type=jnp.float32)
     token_total = lax.axis_size("dp") * seq_count * shard_len
-    weight_grad = lax.psum(weight_acc, ("dp", "seq")) * (1.0 / math.sqrt(token_total))
+    dp_index = lax.axis_index("dp")
+    half_rows = width_cols // 2
+    mine = lax.dynamic_slice_in_dim(weight_acc, dp_index * half_rows, half_rows, axis=0)
+    theirs = lax.dynamic_slice_in_dim(weight_acc, (1 - dp_index) * half_rows, half_rows, axis=0)
+    mine = mine + lax.ppermute(theirs, "dp", [(0, 1), (1, 0)])
+    mine = lax.psum(mine, "seq") * (1.0 / math.sqrt(token_total))
+    other = lax.ppermute(mine, "dp", [(0, 1), (1, 0)])
+    weight_grad = jnp.where(
+        dp_index == 0,
+        jnp.concatenate([mine, other], axis=0),
+        jnp.concatenate([other, mine], axis=0),
+    )
     grad_blocks = grad_piece.reshape(block_count, block_len, head_count, head_dim)
     delta_rows = jnp.sum(grad_blocks.astype(jnp.float32) * attn.astype(jnp.float32), axis=-1)
     row_delta = jnp.transpose(delta_rows, (2, 0, 1))[..., None]
@@ -287,11 +299,12 @@
     grad_k = core[:, :, 0].reshape(shard_len, width_cols).astype(jnp.bfloat16)
     grad_v = core[:, :, 1].reshape(shard_len, width_cols).astype(jnp.bfloat16)
     grad_q_rows = grad_q.reshape(shard_len, width_cols)
-    grad_queries, grad_keys, grad_values = (
-        lax.all_to_all(grad_q_rows[None], "head", split_axis=1, concat_axis=2, tiled=True),
-        lax.all_to_all(grad_k[None], "head", split_axis=1, concat_axis=2, tiled=True),
-        lax.all_to_all(grad_v[None], "head", split_axis=1, concat_axis=2, tiled=True),
-    )
+    back = jnp.stack([grad_q_rows, grad_k, grad_v]).reshape(3, group_count, piece_len, width_cols)
+    back = lax.all_to_all(
+        jnp.transpose(back, (1, 0, 2, 3)), "head", split_axis=0, concat_axis=0, tiled=True
+    )
+    back = jnp.transpose(back, (1, 2, 0, 3)).reshape(3, 1, piece_len, group_count * width_cols)
+    grad_queries, grad_keys, grad_values = back[0], back[1], back[2]
     return (layer_out, grad_queries, grad_keys, grad_values, weight_grad)
 
 

time: 657 us -> 622 us (0.947)
  the two profiles are of different devices: /device:TPU:0 before, /device:TPU:1 now
where the time goes in v2:
time: 622 us; the launch traced here: 615 us
  waiting for transfers between devices  246 us (40%)
  local copies, waits for them, and re-layouts  164 us (26%)
  matrix products  71.3 us (11%)
  starting transfers between devices  55.6 us (9%)
  other arithmetic  48.1 us (8%)
  blocking collectives  15.2 us (2%)
  between operations  14.9 us (2%)
    ppermute x4, waiting for transfers between devices, reduce_to_first(): block = block + lax.ppermute(block, axis, pairs)  109 us
    ppermute x4, waiting for transfers between devices, broadcast_first(): got = lax.ppermute(block, axis, pairs)  93.2 us
    unnamed x78, local copies, waits for them, and re-layouts  70 us
    all_to_all x1, waiting for transfers between devices, per_device(): lax.all_to_all(stacked, 'head', split_axis=0, concat_axis=0, tiled=True)  22.4 us
    all_to_all x1, waiting for transfers between devices, per_device(): lax.all_to_all(jnp.transpose(back, (1, 0, 2, 3)), 'head', split_axis=0, c...  19.8 us
    all_to_all x1, blocking collectives, per_device(): lax.all_to_all(asked_codes, 'seq', split_axis=0, concat_axis=0, tiled=True)  15.2 us
    dot_general x1, local copies, waits for them, and re-layouts, per_device(): jnp.dot(serve_hot.T, incoming.reshape(slot_total, -1), preferred_element_...  13.8 us
  transfers between devices with their start and end apart: 21, of which 7 were waited for; matrix products, arithmetic and copies ran while one was open for 31% of the time, Pallas kernels for 0%

profile of v2, /device:TPU:1, one launch (start us, length us, event | category | flops | bytes accessed | tf_op | source)
XLA Modules:
  0.0 614.9 jit_solution(10211735258695703523)
XLA Ops:
  10.3 5.3 reshape.561
  18.8 5.1 all-to-all-start
  26.0 22.4 %all-to-all-done = bf16[4,3,160,512]{3,2,1,0:T(8,128)(2,1)} async-done(((bf16[4,3,160,512]{3,2,1,0:T(8,128)(2,1)}), bf16[4,3,160,512]{3,2,1,0:T(8,128)(2,1)}, u32[]{:S(2)}, u32[]{:S(2)}) %all-to-all-start) | async-done | bytes 1966112 | tf_op jit(solution)/shard_map/all_to_all | solution.py:59
  59.3 15.2 %all_to_all.29 = s32[16,1,15]{2,1,0:T(1,128)S(1)} all-to-all(s32[16,1,15]{2,1,0:T(1,128)S(1)} %bitcast.261), channel_id=1, replica_groups=mesh['dp'=2,'seq'=16,'head'=4] {'seq'}, dimensions={0} | all-to-all | bytes 1920 | tf_op jit(solution)/shard_map/all_to_all | solution.py:84
  90.3 5.3 convolution_convert_fusion.1
  95.6 8.7 %copy.252 = bf16[30,8,64,256]{3,2,1,0:T(8,128)(2,1)} copy(bf16[30,8,64,256]{3,1,2,0:T(8,128)(2,1)} %bitcast.229) | data formatting | bytes 15728640
  117.9 93.2 %collective-permute-done.2 = bf16[64,1024]{1,0:T(8,128)(2,1)} collective-permute-done((bf16[64,1024]{1,0:T(8,128)(2,1)S(1)}, bf16[64,1024]{1,0:T(8,128)(2,1)}, u32[]{:S(2)}, u32[]{:S(2)}) %collective-permute-start.2) | collective-permute-done | bytes 131104 | tf_op jit(solution)/shard_map/ppermute | solution.py:31
  220.5 4.9 pad_maximum_fusion.1
  242.9 14.4 %copy.253 = bf16[30,8,64,256]{3,1,2,0:T(8,128)(2,1)} copy(bf16[30,8,64,256]{3,2,1,0:T(8,128)(2,1)} %bitcast.99) | data formatting | bytes 15728640
  281.9 5.9 collective-permute-start.12
  288.5 5.0 multiply_convert_fusion.1
  312.3 6.1 copy.256
  322.2 8.2 %convolution_convert_fusion = bf16[240,16384]{1,0:T(8,128)(2,1)} fusion(bf16[160,16384]{1,0:T(8,128)(2,1)} %bitcast.235, s32[160]{0:T(256)S(1)} %multiply_add_fusion.1), kind=kOutput, calls=%fused_computation.1 | convolution fusion | flops 1262261760 | bytes 13107840 | tf_op jit(solution)/shard_map/dot_general | solution.py:290
  330.4 8.7 %copy.257 = bf16[30,8,64,256]{3,2,1,0:T(8,128)(2,1)} copy(bf16[30,8,64,256]{3,1,2,0:T(8,128)(2,1)} %bitcast.228) | data formatting | bytes 15728640
  339.1 9.5 %all-to-all-start.3 = ((bf16[16,15,64,256]{3,2,1,0:T(8,128)(2,1)}), bf16[16,15,64,256]{3,2,1,0:T(8,128)(2,1)}, u32[]{:S(2)}, u32[]{:S(2)}) async-start(bf16[16,15,64,256]{3,2,1,0:T(8,128)(2,1)} %bitcast.231), calls=%async_computation.4 | async-start | bytes 15728640 | tf_op jit(solution)/shard_map/all_to_all | solution.py:294
  370.9 63.3 %collective-permute-done.6 = f32[64,1024]{1,0:T(8,128)S(1)} collective-permute-done((f32[64,1024]{1,0:T(8,128)}, f32[64,1024]{1,0:T(8,128)S(1)}, u32[]{:S(2)}, u32[]{:S(2)}) %collective-permute-start.6) | collective-permute-done | bytes 262176 | tf_op jit(solution)/shard_map/ppermute | solution.py:44
  437.7 11.8 %collective-permute-done.7 = f32[64,1024]{1,0:T(8,128)S(1)} collective-permute-done((f32[64,1024]{1,0:T(8,128)S(1)}, f32[64,1024]{1,0:T(8,128)S(1)}, u32[]{:S(2)}, u32[]{:S(2)}) %collective-permute-start.7) | collective-permute-done | bytes 262176 | tf_op jit(solution)/shard_map/ppermute | solution.py:44
  452.9 28.8 %collective-permute-done.8 = f32[64,1024]{1,0:T(8,128)S(1)} collective-permute-done((f32[64,1024]{1,0:T(8,128)S(1)}, f32[64,1024]{1,0:T(8,128)S(1)}, u32[]{:S(2)}, u32[]{:S(2)}) %collective-permute-start.8) | collective-permute-done | bytes 262176 | tf_op jit(solution)/shard_map/ppermute | solution.py:44
  485.1 5.5 collective-permute-done.9
  524.0 14.4 %copy.258 = bf16[30,8,64,256]{3,1,2,0:T(8,128)(2,1)} copy(bf16[30,8,64,256]{3,2,1,0:T(8,128)(2,1)} %bitcast.114) | data formatting | bytes 15728640
  538.4 13.8 %dot_general.103 = bf16[64,2,128,240]{2,1,0,3:T(2,128)(2,1)} reshape(bf16[16384,240]{0,1:T(8,128)(2,1)} %bitcast.233) | data formatting | bytes 15728640 | tf_op jit(solution)/shard_map/dot_general | solution.py:295
  552.2 10.1 %fusion.6 = bf16[10,64,2,4,128]{4,0,2,1,3:T(8,128)(2,1)S(1)} fusion(f32[10,64,2,4,128]{4,3,2,1,0:T(4,128)} %reshape.578, bf16[64,2,128,240]{2,1,0,3:T(2,128)(2,1)} %dot_general.103, s32[10,4]{0,1:T(4,128)S(1)} %multiply_add_fusion, s32[240]{0:T(256)S(1)} %eq.88), kind=kOutput, calls=%fused_computation.17 | convolution fusion | flops 315893120 | bytes 11797600 | tf_op jit(solution)/shard_map/dot_general | solution.py:295
  576.7 5.1 maximum_select_fusion
  581.8 19.8 %all-to-all-done.4 = bf16[4,3,160,512]{3,2,1,0:T(8,128)(2,1)} async-done(((bf16[4,3,160,512]{3,2,1,0:T(8,128)(2,1)}), bf16[4,3,160,512]{3,2,1,0:T(8,128)(2,1)}, u32[]{:S(2)}, u32[]{:S(2)}) %all-to-all-start.4) | async-done | bytes 1966112 | tf_op jit(solution)/shard_map/all_to_all | solution.py:303
  (241 shorter events, 209.6 us)
Async XLA Ops:
  7.2 229.8 %copy-start = (bf16[512,2048]{1,0:T(8,128)(2,1)S(1)}, bf16[512,2048]{1,0:T(8,128)(2,1)}, u32[]{:S(2)}) copy-start(bf16[512,2048]{1,0:T(8,128)(2,1)} %param.22) | copy-start | bytes 6291460
  18.8 29.6 %all-to-all-start = ((bf16[4,3,160,512]{3,2,1,0:T(8,128)(2,1)}), bf16[4,3,160,512]{3,2,1,0:T(8,128)(2,1)}, u32[]{:S(2)}, u32[]{:S(2)}) async-start(bf16[4,3,160,512]{3,2,1,0:T(8,128)(2,1)} %copy.154), calls=%async_computation | async-start | bytes 3932160 | tf_op jit(solution)/shard_map/all_to_all | solution.py:59
  26.0 32.2 %copy-start.33 = (s32[160]{0:T(256)}, s32[160]{0:T(256)S(1)}, u32[]{:S(2)}) copy-start(s32[160]{0:T(256)S(1)} %fusion.131) | copy-start | bytes 1924
  52.2 23.6 %collective-permute-start.1 = (bf16[64,1024]{1,0:T(8,128)(2,1)S(1)}, bf16[64,1024]{1,0:T(8,128)(2,1)S(1)}, u32[]{:S(2)}, u32[]{:S(2)}) collective-permute-start(bf16[64,1024]{1,0:T(8,128)(2,1)S(1)} %get-tuple-element.103), channel_id=1, source_target_pairs={{4,0},{8,4},{12,8},{16,12},{20,16},{24,20},{28,24},{32,28},{36,32}... | collective-permute-start | bytes 393224 | tf_op jit(solution)/shard_map/ppermute | solution.py:20
  53.5 23.0 %collective-permute-start = (bf16[64,1024]{1,0:T(8,128)(2,1)S(1)}, bf16[64,1024]{1,0:T(8,128)(2,1)}, u32[]{:S(2)}, u32[]{:S(2)}) collective-permute-start(bf16[64,1024]{1,0:T(8,128)(2,1)S(1)} %get-tuple-element.102), channel_id=1, source_target_pairs={{0,4},{4,8},{8,12},{12,16},{16,20},{20,24},{24,28},{28,32},{32,36}... | collective-permute-start | bytes 393224 | tf_op jit(solution)/shard_map/ppermute | solution.py:17
  104.2 138.7 %all-to-all-start.2 = ((bf16[16,15,64,256]{3,2,1,0:T(8,128)(2,1)}), bf16[16,15,64,256]{3,2,1,0:T(8,128)(2,1)}, u32[]{:S(2)}, u32[]{:S(2)}) async-start(bf16[16,15,64,256]{3,2,1,0:T(8,128)(2,1)} %bitcast.232), calls=%async_computation.2 | async-start | bytes 15728640 | tf_op jit(solution)/shard_map/all_to_all | solution.py:99
  109.1 127.9 %all-gather.2.cloned.1.call-start = ((), (), s32[]{:S(2)}) async-start(), calls=%async_computation.7 | async-start | bytes 3276800 | tf_op jit(solution)/shard_map/all_gather | solution.py:173
  109.8 410.1 %all-reduce.4.cloned.1.call-start = ((), (), s32[]{:S(2)}) async-start(), calls=%async_computation.8 | async-start | bytes 4194304 | tf_op jit(solution)/shard_map/psum | solution.py:184
  110.2 100.9 %collective-permute-start.2 = (bf16[64,1024]{1,0:T(8,128)(2,1)S(1)}, bf16[64,1024]{1,0:T(8,128)(2,1)}, u32[]{:S(2)}, u32[]{:S(2)}) collective-permute-start(bf16[64,1024]{1,0:T(8,128)(2,1)S(1)} %get-tuple-element.103), channel_id=1, source_target_pairs={{0,4},{1,5},{2,6},{3,7},{64,68},{65,69},{66,70},{67,71}} | collective-permute-start | bytes 393224 | tf_op jit(solution)/shard_map/ppermute | solution.py:31
  211.1 15.4 %collective-permute-start.3 = (bf16[64,1024]{1,0:T(8,128)(2,1)S(1)}, bf16[64,1024]{1,0:T(8,128)(2,1)S(1)}, u32[]{:S(2)}, u32[]{:S(2)}) collective-permute-start(bf16[64,1024]{1,0:T(8,128)(2,1)S(1)} %broadcast_select_fusion), channel_id=1, source_target_pairs={{0,8},{4,12},{1,9},{5,13},{2,10},{6,14},{3,11},{7,15},{64,72},{68,... | collective-permute-start | bytes 393224 | tf_op jit(solution)/shard_map/ppermute | solution.py:31
  226.5 3.5 collective-permute-start.4
  230.0 4.3 collective-permute-start.5
  281.9 16.3 %collective-permute-start.12 = (f32[256,2048]{1,0:T(8,128)}, f32[256,2048]{1,0:T(8,128)}, u32[]{:S(2)}, u32[]{:S(2)}) collective-permute-start(f32[256,2048]{1,0:T(8,128)} %constant_dynamic-slice_fusion), channel_id=1, source_target_pairs={{0,64},{64,0},{1,65},{65,1},{2,66},{66,2},{3,67},{67,3},{4,68},{68... | collective-permute-start | bytes 6291464 | tf_op jit(solution)/shard_map/ppermute | solution.py:183
  301.4 304.5 %reduce-scatter.2.cloned.1.call-start = ((), (), s32[]{:S(2)}) async-start(), calls=%async_computation.6 | async-start | bytes 6553600 | tf_op jit(solution)/shard_map/reduce_scatter | solution.py:167
  339.1 184.9 %all-to-all-start.3 = ((bf16[16,15,64,256]{3,2,1,0:T(8,128)(2,1)}), bf16[16,15,64,256]{3,2,1,0:T(8,128)(2,1)}, u32[]{:S(2)}, u32[]{:S(2)}) async-start(bf16[16,15,64,256]{3,2,1,0:T(8,128)(2,1)} %bitcast.231), calls=%async_computation.4 | async-start | bytes 15728640 | tf_op jit(solution)/shard_map/all_to_all | solution.py:294
  351.1 83.0 %collective-permute-start.6 = (f32[64,1024]{1,0:T(8,128)}, f32[64,1024]{1,0:T(8,128)S(1)}, u32[]{:S(2)}, u32[]{:S(2)}) collective-permute-start(f32[64,1024]{1,0:T(8,128)} %reshape.575), channel_id=1, source_target_pairs={{32,0},{36,4},{40,8},{44,12},{48,16},{52,20},{56,24},{60,28},{33,1... | collective-permute-start | bytes 786440 | tf_op jit(solution)/shard_map/ppermute | solution.py:44
  435.1 15.7 %copy-start.5 = (bf16[10,4,4,64,128]{4,3,2,1,0:T(8,128)(2,1)S(1)}, bf16[10,4,4,64,128]{4,3,2,1,0:T(8,128)(2,1)}, u32[]{:S(2)}) copy-start(bf16[10,4,4,64,128]{4,3,2,1,0:T(8,128)(2,1)} %copy-done.4) | copy-start | bytes 7864324
  435.2 14.3 %collective-permute-start.7 = (f32[64,1024]{1,0:T(8,128)S(1)}, f32[64,1024]{1,0:T(8,128)S(1)}, u32[]{:S(2)}, u32[]{:S(2)}) collective-permute-start(f32[64,1024]{1,0:T(8,128)S(1)} %add.237), channel_id=1, source_target_pairs={{16,0},{20,4},{24,8},{28,12},{17,1},{21,5},{25,9},{29,13},{18,2},{... | collective-permute-start | bytes 786440 | tf_op jit(solution)/shard_map/ppermute | solution.py:44
  449.5 32.2 %collective-permute-start.8 = (f32[64,1024]{1,0:T(8,128)S(1)}, f32[64,1024]{1,0:T(8,128)S(1)}, u32[]{:S(2)}, u32[]{:S(2)}) collective-permute-start(f32[64,1024]{1,0:T(8,128)S(1)} %add.238), channel_id=1, source_target_pairs={{8,0},{12,4},{9,1},{13,5},{10,2},{14,6},{11,3},{15,7},{72,64},{76,... | collective-permute-start | bytes 786440 | tf_op jit(solution)/shard_map/ppermute | solution.py:44
  481.8 8.8 %collective-permute-start.9 = (f32[64,1024]{1,0:T(8,128)S(1)}, f32[64,1024]{1,0:T(8,128)S(1)}, u32[]{:S(2)}, u32[]{:S(2)}) collective-permute-start(f32[64,1024]{1,0:T(8,128)S(1)} %add.239), channel_id=1, source_target_pairs={{4,0},{5,1},{6,2},{7,3},{68,64},{69,65},{70,66},{71,67}} | collective-permute-start | bytes 786440 | tf_op jit(solution)/shard_map/ppermute | solution.py:44
  496.0 16.4 %collective-permute-start.10 = (bf16[64,1024]{1,0:T(8,128)(2,1)S(1)}, bf16[64,1024]{1,0:T(8,128)(2,1)}, u32[]{:S(2)}, u32[]{:S(2)}) collective-permute-start(bf16[64,1024]{1,0:T(8,128)(2,1)S(1)} %concatenate.51), channel_id=1, source_target_pairs={{0,4},{4,8},{8,12},{12,16},{16,20},{20,24},{24,28},{28,32},{32,36}... | collective-permute-start | bytes 393224 | tf_op jit(solution)/shard_map/ppermute | solution.py:17
  498.9 13.5 %collective-permute-start.11 = (bf16[64,1024]{1,0:T(8,128)(2,1)S(1)}, bf16[64,1024]{1,0:T(8,128)(2,1)}, u32[]{:S(2)}, u32[]{:S(2)}) collective-permute-start(bf16[64,1024]{1,0:T(8,128)(2,1)S(1)} %concatenate.52), channel_id=1, source_target_pairs={{4,0},{8,4},{12,8},{16,12},{20,16},{24,20},{28,24},{32,28},{36,32}... | collective-permute-start | bytes 393224 | tf_op jit(solution)/shard_map/ppermute | solution.py:20
  521.8 54.8 %collective-permute-start.13 = (f32[256,2048]{1,0:T(8,128)S(1)}, f32[256,2048]{1,0:T(8,128)}, u32[]{:S(2)}, u32[]{:S(2)}) collective-permute-start(f32[256,2048]{1,0:T(8,128)S(1)} %broadcast_multiply_fusion), channel_id=1, source_target_pairs={{0,64},{64,0},{1,65},{65,1},{2,66},{66,2},{3,67},{67,3},{4,68},{68... | collective-permute-start | bytes 6291464 | tf_op jit(solution)/shard_map/ppermute | solution.py:185
  572.2 29.4 %all-to-all-start.4 = ((bf16[4,3,160,512]{3,2,1,0:T(8,128)(2,1)}), bf16[4,3,160,512]{3,2,1,0:T(8,128)(2,1)}, u32[]{:S(2)}, u32[]{:S(2)}) async-start(bf16[4,3,160,512]{3,2,1,0:T(8,128)(2,1)} %copy.214), calls=%async_computation.5 | async-start | bytes 3932160 | tf_op jit(solution)/shard_map/all_to_all | solution.py:303
  (32 other events, 155.7 us)
Sparse Core Ops, SparseCore 0:
  111.6 37.4 all-gather.1
  301.6 171.8 all-reduce.3
  475.8 58.8 reduce-scatter.1

commit v3 on v2

--- a/solution.py
+++ b/solution.py
@@ -92,14 +92,20 @@
         slot_of[:, None] == jnp.arange(slot_total, dtype=jnp.int32)[None, :]
     ).astype(jnp.bfloat16)
     kv_pairs = jnp.transpose(
-        key_value.reshape(block_count, block_len, 2, head_count, head_dim), (0, 3, 1, 2, 4)
-    ).reshape(pair_count, block_len * 2 * head_dim)
-    served = jnp.dot(serve_hot, kv_pairs, preferred_element_type=jnp.float32).astype(jnp.bfloat16)
-    served = served.reshape(seq_count, capacity, block_len, 2 * head_dim)
-    received = lax.all_to_all(served, "seq", split_axis=0, concat_axis=0, tiled=True)
-    far_pairs = jnp.dot(
-        pick_hot, received.reshape(slot_total, -1), preferred_element_type=jnp.float32
-    ).astype(jnp.bfloat16)
+        key_value.reshape(block_count, block_len, 2, head_count, head_dim), (2, 0, 3, 1, 4)
+    ).reshape(2, pair_count, block_len * head_dim)
+
+    def fetch(pairs):
+        served = jnp.dot(serve_hot, pairs, preferred_element_type=jnp.float32).astype(jnp.bfloat16)
+        served = served.reshape(seq_count, capacity, block_len, head_dim)
+        received = lax.all_to_all(served, "seq", split_axis=0, concat_axis=0, tiled=True)
+        picked = jnp.dot(
+            pick_hot, received.reshape(slot_total, -1), preferred_element_type=jnp.float32
+        ).astype(jnp.bfloat16)
+        return picked.reshape(block_count, rand_count, head_count, block_len, head_dim)
+
+    far_keys = fetch(kv_pairs[0])
+    far_vals = fetch(kv_pairs[1])
     pair_view = padded.reshape(block_count + 2, block_len, 2, head_count, head_dim)
     window_pairs = jnp.stack(
         [pair_view[:block_count], pair_view[1 : block_count + 1], pair_view[2:]], axis=1
@@ -109,9 +115,6 @@
     first_pairs = first_block.reshape(block_len, 2, head_count, head_dim)
     first_keys = first_pairs[:, 0]
     first_vals = first_pairs[:, 1]
-    far_view = far_pairs.reshape(block_count, rand_count, head_count, block_len, 2 * head_dim)
-    far_keys = far_view[..., :head_dim]
-    far_vals = far_view[..., head_dim:]
     global_ids = seq_index * block_count + jnp.arange(block_count, dtype=jnp.int32)
     block_total = seq_count * block_count
     window_live = jnp.stack([global_ids > 0, global_ids >= 0, global_ids < block_total - 1], axis=1)
@@ -282,19 +285,20 @@
         .add(rim_sums[3 * block_len :])
     )
     core = core.reshape(block_count, block_len, 2, head_count, head_dim)
-    far_terms = (
-        jnp.concatenate([key_far, value_far], axis=-1)
-        .reshape(request_count, block_len * 2 * head_dim)
-        .astype(jnp.bfloat16)
-    )
-    outgoing = jnp.dot(pick_hot.T, far_terms, preferred_element_type=jnp.float32).astype(
-        jnp.bfloat16
-    )
-    outgoing = outgoing.reshape(seq_count, capacity, block_len, 2 * head_dim)
-    incoming = lax.all_to_all(outgoing, "seq", split_axis=0, concat_axis=0, tiled=True)
-    added = jnp.dot(
-        serve_hot.T, incoming.reshape(slot_total, -1), preferred_element_type=jnp.float32
-    ).reshape(block_count, head_count, block_len, 2, head_dim)
+    def give_back(terms):
+        terms = terms.reshape(request_count, block_len * head_dim).astype(jnp.bfloat16)
+        outgoing = jnp.dot(pick_hot.T, terms, preferred_element_type=jnp.float32).astype(
+            jnp.bfloat16
+        )
+        outgoing = outgoing.reshape(seq_count, capacity, block_len, head_dim)
+        incoming = lax.all_to_all(outgoing, "seq", split_axis=0, concat_axis=0, tiled=True)
+        return jnp.dot(
+            serve_hot.T, incoming.reshape(slot_total, -1), preferred_element_type=jnp.float32
+        ).reshape(block_count, head_count, block_len, head_dim)
+
+    added_vals = give_back(value_far)
+    added_keys = give_back(key_far)
+    added = jnp.stack([added_keys, added_vals], axis=3)
     core = core + jnp.transpose(added, (0, 2, 3, 1, 4))
     grad_k = core[:, :, 0].reshape(shard_len, width_cols).astype(jnp.bfloat16)
     grad_v = core[:, :, 1].reshape(shard_len, width_cols).astype(jnp.bfloat16)

time: 622 us -> 548 us (0.88)
  local copies, waits for them, and re-layouts: 164 us -> 108 us
  waiting for transfers between devices: 246 us -> 203 us
  starting transfers between devices: 55.6 us -> 69.8 us
  other arithmetic: 48.1 us -> 56.1 us
    ppermute x4, waiting for transfers between devices: 93.2 us -> 29.8 us  [broadcast_first(): got = lax.ppermute(block, axis, pairs)]
    all_to_all x2 -> x4, waiting for transfers between devices: 0.01 us -> 59.6 us  [the longest x2 40.4 us: fetch(): lax.all_to_all(served, 'seq', split_axis=0, concat_axis=0, tiled=True)]
    ppermute x4, waiting for transfers between devices: 109 us -> 55.6 us  [reduce_to_first(): block = block + lax.ppermute(block, axis, pairs)]
    unnamed x78 -> x88, local copies, waits for them, and re-layouts: 70 us -> 30.4 us
    all_to_all x1, waiting for transfers between devices: 19.8 us -> 35.2 us  [per_device(): lax.all_to_all(jnp.transpose(back, (1, 0, 2, 3)), 'head', split_axis=0, c...]
    dot_general x1 -> x0, local copies, waits for them, and re-layouts: 13.8 us -> none  [per_device(): jnp.dot(serve_hot.T, incoming.reshape(slot_total, -1), preferred_element_...]
    all_to_all x2 -> x4, starting transfers between devices: 14.3 us -> 28.1 us  [the longest x2 16.7 us: give_back(): lax.all_to_all(outgoing, 'seq', split_axis=0, concat_axis=0, tiled=True)]
    dot_general x4 -> x8, matrix products: 28.3 us -> 28.8 us  [the longest x2 10.6 us: give_back(): jnp.dot(serve_hot.T, incoming.reshape(slot_total, -1), preferred_element_...]
  transfers between devices with their start and end apart: 21 -> 23, of which waited for: 7 -> 9; matrix products, arithmetic and copies ran while one was open for 31% -> 33% of each run, Pallas kernels for 0% -> 0%
where the time goes in v3:
time: 548 us; the launch traced here: 537 us
  waiting for transfers between devices  203 us (37%)
  local copies, waits for them, and re-layouts  108 us (20%)
  matrix products  70.3 us (13%)
  starting transfers between devices  69.8 us (13%)
  other arithmetic  56.1 us (10%)
  blocking collectives  15.1 us (3%)
  between operations  15 us (3%)
    ppermute x4, waiting for transfers between devices, reduce_to_first(): block = block + lax.ppermute(block, axis, pairs)  55.6 us
    all_to_all x2, waiting for transfers between devices, fetch(): lax.all_to_all(served, 'seq', split_axis=0, concat_axis=0, tiled=True)  40.4 us
    all_to_all x1, waiting for transfers between devices, per_device(): lax.all_to_all(jnp.transpose(back, (1, 0, 2, 3)), 'head', split_axis=0, c...  35.2 us
    unnamed x88, local copies, waits for them, and re-layouts  30.4 us
    ppermute x4, waiting for transfers between devices, broadcast_first(): got = lax.ppermute(block, axis, pairs)  29.8 us
    all_to_all x1, waiting for transfers between devices, per_device(): lax.all_to_all(stacked, 'head', split_axis=0, concat_axis=0, tiled=True)  22.4 us
    all_to_all x2, waiting for transfers between devices, give_back(): lax.all_to_all(outgoing, 'seq', split_axis=0, concat_axis=0, tiled=True)  19.2 us
    all_to_all x2, starting transfers between devices, give_back(): lax.all_to_all(outgoing, 'seq', split_axis=0, concat_axis=0, tiled=True)  16.7 us
  transfers between devices with their start and end apart: 23, of which 9 were waited for; matrix products, arithmetic and copies ran while one was open for 33% of the time, Pallas kernels for 0%

profile of v3, /device:TPU:1, one launch (start us, length us, event | category | flops | bytes accessed | tf_op | source)
XLA Modules:
  0.0 537.3 jit_solution(10719707984748581135)
XLA Ops:
  10.3 5.3 reshape.592
  18.8 5.1 all-to-all-start
  26.0 22.4 %all-to-all-done = bf16[4,3,160,512]{3,2,1,0:T(8,128)(2,1)} async-done(((bf16[4,3,160,512]{3,2,1,0:T(8,128)(2,1)}), bf16[4,3,160,512]{3,2,1,0:T(8,128)(2,1)}, u32[]{:S(2)}, u32[]{:S(2)}) %all-to-all-start) | async-done | bytes 1966112 | tf_op jit(solution)/shard_map/all_to_all | solution.py:59
  57.9 15.1 %all_to_all.39 = s32[16,1,15]{2,1,0:T(1,128)S(1)} all-to-all(s32[16,1,15]{2,1,0:T(1,128)S(1)} %bitcast.347), channel_id=1, replica_groups=mesh['dp'=2,'seq'=16,'head'=4] {'seq'}, dimensions={0} | all-to-all | bytes 1920 | tf_op jit(solution)/shard_map/all_to_all | solution.py:84
  101.4 40.4 %all-to-all-done.2 = bf16[16,15,64,128]{3,2,1,0:T(8,128)(2,1)} async-done(((bf16[16,15,64,128]{3,2,1,0:T(8,128)(2,1)}), bf16[16,15,64,128]{3,2,1,0:T(8,128)(2,1)}, u32[]{:S(2)}, u32[]{:S(2)}) %all-to-all-start.2) | async-done | bytes 3932192 | tf_op jit(solution)/shard_map/all_to_all | solution.py:101
  141.8 6.9 %all-to-all-start.3 = ((bf16[16,15,64,128]{3,2,1,0:T(8,128)(2,1)}), bf16[16,15,64,128]{3,2,1,0:T(8,128)(2,1)}, u32[]{:S(2)}, u32[]{:S(2)}) async-start(bf16[16,15,64,128]{3,2,1,0:T(8,128)(2,1)} %bitcast.323), calls=%async_computation.3 | async-start | bytes 7864320 | tf_op jit(solution)/shard_map/all_to_all | solution.py:101
  153.1 5.9 %collective-permute-start.3 = (bf16[64,1024]{1,0:T(8,128)(2,1)S(1)}, bf16[64,1024]{1,0:T(8,128)(2,1)S(1)}, u32[]{:S(2)}, u32[]{:S(2)}) collective-permute-start(bf16[64,1024]{1,0:T(8,128)(2,1)S(1)} %broadcast_select_fusion), channel_id=1, source_target_pairs={{0,8},{4,12},{1,9},{5,13},{2,10},{6,14},{3,11},{7,15},{64,72},{68,... | collective-permute-start | bytes 393224 | tf_op jit(solution)/shard_map/ppermute | solution.py:31
  166.6 4.9 pad_maximum_fusion
  172.5 26.3 %collective-permute-done.3 = bf16[64,1024]{1,0:T(8,128)(2,1)S(1)} collective-permute-done((bf16[64,1024]{1,0:T(8,128)(2,1)S(1)}, bf16[64,1024]{1,0:T(8,128)(2,1)S(1)}, u32[]{:S(2)}, u32[]{:S(2)}) %collective-permute-start.3) | collective-permute-done | bytes 131104 | tf_op jit(solution)/shard_map/ppermute | solution.py:31
  219.1 4.8 fusion.52
  226.2 4.8 fusion.55
  269.0 12.2 %all-to-all-start.5 = ((bf16[16,15,64,128]{3,2,1,0:T(8,128)(2,1)}), bf16[16,15,64,128]{3,2,1,0:T(8,128)(2,1)}, u32[]{:S(2)}, u32[]{:S(2)}) async-start(bf16[16,15,64,128]{3,2,1,0:T(8,128)(2,1)} %bitcast.324), calls=%async_computation.6 | async-start | bytes 7864320 | tf_op jit(solution)/shard_map/all_to_all | solution.py:294
  295.1 5.0 fusion.113
  315.6 5.3 copy_dynamic-update-slice_fusion.1
  321.0 5.3 copy_dynamic-update-slice_fusion
  326.3 19.2 %all-to-all-done.5 = bf16[16,15,64,128]{3,2,1,0:T(8,128)(2,1)} async-done(((bf16[16,15,64,128]{3,2,1,0:T(8,128)(2,1)}), bf16[16,15,64,128]{3,2,1,0:T(8,128)(2,1)}, u32[]{:S(2)}, u32[]{:S(2)}) %all-to-all-start.5) | async-done | bytes 3932192 | tf_op jit(solution)/shard_map/all_to_all | solution.py:294
  361.1 39.6 %collective-permute-done.7 = f32[64,1024]{1,0:T(8,128)S(1)} collective-permute-done((f32[64,1024]{1,0:T(8,128)S(1)}, f32[64,1024]{1,0:T(8,128)S(1)}, u32[]{:S(2)}, u32[]{:S(2)}) %collective-permute-start.7) | collective-permute-done | bytes 262176 | tf_op jit(solution)/shard_map/ppermute | solution.py:44
  404.3 10.5 %collective-permute-done.8 = f32[64,1024]{1,0:T(8,128)S(1)} collective-permute-done((f32[64,1024]{1,0:T(8,128)S(1)}, f32[64,1024]{1,0:T(8,128)S(1)}, u32[]{:S(2)}, u32[]{:S(2)}) %collective-permute-start.8) | collective-permute-done | bytes 262176 | tf_op jit(solution)/shard_map/ppermute | solution.py:44
  417.6 5.6 %collective-permute-done.9 = f32[64,1024]{1,0:T(8,128)S(1)} collective-permute-done((f32[64,1024]{1,0:T(8,128)S(1)}, f32[64,1024]{1,0:T(8,128)S(1)}, u32[]{:S(2)}, u32[]{:S(2)}) %collective-permute-start.9) | collective-permute-done | bytes 262176 | tf_op jit(solution)/shard_map/ppermute | solution.py:44
  431.0 4.7 collective-permute-start.10
  455.5 5.9 %fusion.59 = f32[10,4,64,1,128]{4,0,2,1,3:T(8,128)} fusion(s32[10,4]{0,1:T(4,128)S(1)} %multiply_add_fusion, s32[240]{0:T(256)S(1)} %eq.89, bf16[30,8,64,128]{3,2,1,0:T(8,128)(2,1)} %bitcast.146), kind=kOutput, calls=%fused_computation.90 | convolution fusion | flops 157296000 | bytes 5244000 | tf_op jit(solution)/shard_map/dot_general | solution.py:295
  461.3 4.7 fusion.58
  483.6 35.2 %all-to-all-done.6 = bf16[4,3,160,512]{3,2,1,0:T(8,128)(2,1)S(1)} async-done(((bf16[4,3,160,512]{3,2,1,0:T(8,128)(2,1)}), bf16[4,3,160,512]{3,2,1,0:T(8,128)(2,1)S(1)}, u32[]{:S(2)}, u32[]{:S(2)}) %all-to-all-start.6) | async-done | bytes 1966112 | tf_op jit(solution)/shard_map/all_to_all | solution.py:307
  521.6 6.7 %maximum_select_fusion = f32[512,2048]{1,0:T(8,128)} fusion(f32[256,2048]{1,0:T(8,128)} %collective-permute-done.13, f32[256,2048]{1,0:T(8,128)} %broadcast_multiply_fusion, pred[]{:T(512)S(6)} %eq.102), kind=kLoop, calls=%fused_computation.17 | loop fusion | flops 3145728 | bytes 8388609 | tf_op jit(solution)/shard_map/jit(_where)/select_n | solution.py:189
  (258 shorter events, 220.6 us)
Async XLA Ops:
  7.2 205.7 %copy-start = (bf16[512,2048]{1,0:T(8,128)(2,1)S(1)}, bf16[512,2048]{1,0:T(8,128)(2,1)}, u32[]{:S(2)}) copy-start(bf16[512,2048]{1,0:T(8,128)(2,1)} %param.22) | copy-start | bytes 6291460
  18.8 29.6 %all-to-all-start = ((bf16[4,3,160,512]{3,2,1,0:T(8,128)(2,1)}), bf16[4,3,160,512]{3,2,1,0:T(8,128)(2,1)}, u32[]{:S(2)}, u32[]{:S(2)}) async-start(bf16[4,3,160,512]{3,2,1,0:T(8,128)(2,1)} %copy.158), calls=%async_computation | async-start | bytes 3932160 | tf_op jit(solution)/shard_map/all_to_all | solution.py:59
  52.2 22.0 %collective-permute-start = (bf16[64,1024]{1,0:T(8,128)(2,1)S(1)}, bf16[64,1024]{1,0:T(8,128)(2,1)S(1)}, u32[]{:S(2)}, u32[]{:S(2)}) collective-permute-start(bf16[64,1024]{1,0:T(8,128)(2,1)S(1)} %get-tuple-element.102), channel_id=1, source_target_pairs={{0,4},{4,8},{8,12},{12,16},{16,20},{20,24},{24,28},{28,32},{32,36}... | collective-permute-start | bytes 393224 | tf_op jit(solution)/shard_map/ppermute | solution.py:17
  55.4 19.5 %collective-permute-start.1 = (bf16[64,1024]{1,0:T(8,128)(2,1)S(1)}, bf16[64,1024]{1,0:T(8,128)(2,1)}, u32[]{:S(2)}, u32[]{:S(2)}) collective-permute-start(bf16[64,1024]{1,0:T(8,128)(2,1)S(1)} %get-tuple-element.103), channel_id=1, source_target_pairs={{4,0},{8,4},{12,8},{16,12},{20,16},{24,20},{28,24},{32,28},{36,32}... | collective-permute-start | bytes 393224 | tf_op jit(solution)/shard_map/ppermute | solution.py:20
  87.1 54.7 %all-to-all-start.2 = ((bf16[16,15,64,128]{3,2,1,0:T(8,128)(2,1)}), bf16[16,15,64,128]{3,2,1,0:T(8,128)(2,1)}, u32[]{:S(2)}, u32[]{:S(2)}) async-start(bf16[16,15,64,128]{3,2,1,0:T(8,128)(2,1)} %bitcast.325), calls=%async_computation.2 | async-start | bytes 7864320 | tf_op jit(solution)/shard_map/all_to_all | solution.py:101
  91.7 121.2 %all-gather.2.cloned.1.call-start = ((), (), s32[]{:S(2)}) async-start(), calls=%async_computation.9 | async-start | bytes 3276800 | tf_op jit(solution)/shard_map/all_gather | solution.py:176
  93.5 59.6 %collective-permute-start.2 = (bf16[64,1024]{1,0:T(8,128)(2,1)S(1)}, bf16[64,1024]{1,0:T(8,128)(2,1)}, u32[]{:S(2)}, u32[]{:S(2)}) collective-permute-start(bf16[64,1024]{1,0:T(8,128)(2,1)S(1)} %get-tuple-element.103), channel_id=1, source_target_pairs={{0,4},{1,5},{2,6},{3,7},{64,68},{65,69},{66,70},{67,71}} | collective-permute-start | bytes 393224 | tf_op jit(solution)/shard_map/ppermute | solution.py:31
  141.8 84.4 %all-to-all-start.3 = ((bf16[16,15,64,128]{3,2,1,0:T(8,128)(2,1)}), bf16[16,15,64,128]{3,2,1,0:T(8,128)(2,1)}, u32[]{:S(2)}, u32[]{:S(2)}) async-start(bf16[16,15,64,128]{3,2,1,0:T(8,128)(2,1)} %bitcast.323), calls=%async_computation.3 | async-start | bytes 7864320 | tf_op jit(solution)/shard_map/all_to_all | solution.py:101
  148.7 319.1 %all-reduce.4.cloned.1.call-start = ((), (), s32[]{:S(2)}) async-start(), calls=%async_computation.10 | async-start | bytes 4194304 | tf_op jit(solution)/shard_map/psum | solution.py:187
  153.1 45.7 %collective-permute-start.3 = (bf16[64,1024]{1,0:T(8,128)(2,1)S(1)}, bf16[64,1024]{1,0:T(8,128)(2,1)S(1)}, u32[]{:S(2)}, u32[]{:S(2)}) collective-permute-start(bf16[64,1024]{1,0:T(8,128)(2,1)S(1)} %broadcast_select_fusion), channel_id=1, source_target_pairs={{0,8},{4,12},{1,9},{5,13},{2,10},{6,14},{3,11},{7,15},{64,72},{68,... | collective-permute-start | bytes 393224 | tf_op jit(solution)/shard_map/ppermute | solution.py:31
  198.9 7.0 %collective-permute-start.4 = (bf16[64,1024]{1,0:T(8,128)(2,1)S(1)}, bf16[64,1024]{1,0:T(8,128)(2,1)S(1)}, u32[]{:S(2)}, u32[]{:S(2)}) collective-permute-start(bf16[64,1024]{1,0:T(8,128)(2,1)S(1)} %broadcast_select_fusion.1), channel_id=1, source_target_pairs={{0,16},{4,20},{8,24},{12,28},{1,17},{5,21},{9,25},{13,29},{2,18},{... | collective-permute-start | bytes 393224 | tf_op jit(solution)/shard_map/ppermute | solution.py:31
  205.9 4.3 collective-permute-start.5
  248.2 9.5 %collective-permute-start.12 = (f32[256,2048]{1,0:T(8,128)}, f32[256,2048]{1,0:T(8,128)}, u32[]{:S(2)}, u32[]{:S(2)}) collective-permute-start(f32[256,2048]{1,0:T(8,128)} %constant_dynamic-slice_fusion), channel_id=1, source_target_pairs={{0,64},{64,0},{1,65},{65,1},{2,66},{66,2},{3,67},{67,3},{4,68},{68... | collective-permute-start | bytes 6291464 | tf_op jit(solution)/shard_map/ppermute | solution.py:186
  269.0 76.5 %all-to-all-start.5 = ((bf16[16,15,64,128]{3,2,1,0:T(8,128)(2,1)}), bf16[16,15,64,128]{3,2,1,0:T(8,128)(2,1)}, u32[]{:S(2)}, u32[]{:S(2)}) async-start(bf16[16,15,64,128]{3,2,1,0:T(8,128)(2,1)} %bitcast.324), calls=%async_computation.6 | async-start | bytes 7864320 | tf_op jit(solution)/shard_map/all_to_all | solution.py:294
  281.2 247.2 %reduce-scatter.2.cloned.1.call-start = ((), (), s32[]{:S(2)}) async-start(), calls=%async_computation.8 | async-start | bytes 6553600 | tf_op jit(solution)/shard_map/reduce_scatter | solution.py:170
  293.8 61.8 %collective-permute-start.6 = (f32[64,1024]{1,0:T(8,128)}, f32[64,1024]{1,0:T(8,128)}, u32[]{:S(2)}, u32[]{:S(2)}) collective-permute-start(f32[64,1024]{1,0:T(8,128)} %reshape.608), channel_id=1, source_target_pairs={{32,0},{36,4},{40,8},{44,12},{48,16},{52,20},{56,24},{60,28},{33,1... | collective-permute-start | bytes 786440 | tf_op jit(solution)/shard_map/ppermute | solution.py:44
  345.5 115.9 %all-to-all-start.4 = ((bf16[16,15,64,128]{3,2,1,0:T(8,128)(2,1)}), bf16[16,15,64,128]{3,2,1,0:T(8,128)(2,1)}, u32[]{:S(2)}, u32[]{:S(2)}) async-start(bf16[16,15,64,128]{3,2,1,0:T(8,128)(2,1)} %bitcast.322), calls=%async_computation.5 | async-start | bytes 7864320 | tf_op jit(solution)/shard_map/all_to_all | solution.py:294
  356.6 44.0 %collective-permute-start.7 = (f32[64,1024]{1,0:T(8,128)S(1)}, f32[64,1024]{1,0:T(8,128)S(1)}, u32[]{:S(2)}, u32[]{:S(2)}) collective-permute-start(f32[64,1024]{1,0:T(8,128)S(1)} %add.237), channel_id=1, source_target_pairs={{16,0},{20,4},{24,8},{28,12},{17,1},{21,5},{25,9},{29,13},{18,2},{... | collective-permute-start | bytes 786440 | tf_op jit(solution)/shard_map/ppermute | solution.py:44
  400.7 14.1 %collective-permute-start.8 = (f32[64,1024]{1,0:T(8,128)S(1)}, f32[64,1024]{1,0:T(8,128)S(1)}, u32[]{:S(2)}, u32[]{:S(2)}) collective-permute-start(f32[64,1024]{1,0:T(8,128)S(1)} %add.238), channel_id=1, source_target_pairs={{8,0},{12,4},{9,1},{13,5},{10,2},{14,6},{11,3},{15,7},{72,64},{76,... | collective-permute-start | bytes 786440 | tf_op jit(solution)/shard_map/ppermute | solution.py:44
  414.8 8.3 %collective-permute-start.9 = (f32[64,1024]{1,0:T(8,128)S(1)}, f32[64,1024]{1,0:T(8,128)S(1)}, u32[]{:S(2)}, u32[]{:S(2)}) collective-permute-start(f32[64,1024]{1,0:T(8,128)S(1)} %add.239), channel_id=1, source_target_pairs={{4,0},{5,1},{6,2},{7,3},{68,64},{69,65},{70,66},{71,67}} | collective-permute-start | bytes 786440 | tf_op jit(solution)/shard_map/ppermute | solution.py:44
  429.7 18.1 %collective-permute-start.11 = (bf16[64,1024]{1,0:T(8,128)(2,1)S(1)}, bf16[64,1024]{1,0:T(8,128)(2,1)}, u32[]{:S(2)}, u32[]{:S(2)}) collective-permute-start(bf16[64,1024]{1,0:T(8,128)(2,1)S(1)} %concatenate.48), channel_id=1, source_target_pairs={{4,0},{8,4},{12,8},{16,12},{20,16},{24,20},{28,24},{32,28},{36,32}... | collective-permute-start | bytes 393224 | tf_op jit(solution)/shard_map/ppermute | solution.py:20
  431.0 16.8 %collective-permute-start.10 = (bf16[64,1024]{1,0:T(8,128)(2,1)S(1)}, bf16[64,1024]{1,0:T(8,128)(2,1)}, u32[]{:S(2)}, u32[]{:S(2)}) collective-permute-start(bf16[64,1024]{1,0:T(8,128)(2,1)S(1)} %concatenate.47), channel_id=1, source_target_pairs={{0,4},{4,8},{8,12},{12,16},{16,20},{20,24},{24,28},{28,32},{32,36}... | collective-permute-start | bytes 393224 | tf_op jit(solution)/shard_map/ppermute | solution.py:17
  471.0 50.6 %collective-permute-start.13 = (f32[256,2048]{1,0:T(8,128)}, f32[256,2048]{1,0:T(8,128)}, u32[]{:S(2)}, u32[]{:S(2)}) collective-permute-start(f32[256,2048]{1,0:T(8,128)} %broadcast_multiply_fusion), channel_id=1, source_target_pairs={{0,64},{64,0},{1,65},{65,1},{2,66},{66,2},{3,67},{67,3},{4,68},{68... | collective-permute-start | bytes 6291464 | tf_op jit(solution)/shard_map/ppermute | solution.py:188
  479.8 38.9 %all-to-all-start.6 = ((bf16[4,3,160,512]{3,2,1,0:T(8,128)(2,1)}), bf16[4,3,160,512]{3,2,1,0:T(8,128)(2,1)S(1)}, u32[]{:S(2)}, u32[]{:S(2)}) async-start(bf16[4,3,160,512]{3,2,1,0:T(8,128)(2,1)} %copy.220), calls=%async_computation.7 | async-start | bytes 3932160 | tf_op jit(solution)/shard_map/all_to_all | solution.py:307
  (39 other events, 315.8 us)
Sparse Core Ops, SparseCore 0:
  94.1 37.4 all-gather.1
  262.2 178.0 all-reduce.3
  442.7 65.3 reduce-scatter.1

commit v4 on v3

--- a/solution.py
+++ b/solution.py
@@ -22,28 +22,48 @@
     return block
 
 
-def broadcast_first(block, axis):
+def broadcast_first(block, axis, radix=4):
     count = lax.axis_size(axis)
     index = lax.axis_index(axis)
-    step = 1
-    while step < count:
-        pairs = [(i, i + step) for i in range(step) if i + step < count]
-        got = lax.ppermute(block, axis, pairs)
-        block = jnp.where(index >= step, got, block)
-        step *= 2
+    stride = 1
+    while stride * radix < count:
+        stride *= radix
+    while stride >= 1:
+        span = stride * radix
+        updated = block
+        for m in range(1, radix):
+            pairs = [(j, j + m * stride) for j in range(0, count, span) if j + m * stride < count]
+            if pairs:
+                got = lax.ppermute(block, axis, pairs)
+                updated = jnp.where(index % span == m * stride, got, updated)
+        block = updated
+        stride //= radix
     return block
 
 
-def reduce_to_first(block, axis):
+def reduce_to_first(block, axis, radix=4):
     count = lax.axis_size(axis)
-    step = 1
-    while step * 2 < count:
-        step *= 2
-    while step >= 1:
-        pairs = [(i + step, i) for i in range(step) if i + step < count]
-        block = block + lax.ppermute(block, axis, pairs)
-        step //= 2
+    stride = 1
+    while stride < count:
+        span = stride * radix
+        total = block
+        for m in range(1, radix):
+            pairs = [(j + m * stride, j) for j in range(0, count, span) if j + m * stride < count]
+            if pairs:
+                total = total + lax.ppermute(block, axis, pairs)
+        block = total
+        stride *= radix
     return block
+
+
+def request_slots(rand_blocks, block_count, head_count, seq_count, capacity):
+    requests = jnp.transpose(rand_blocks, (0, 2, 1)).reshape(-1)
+    head_of = jnp.arange(requests.shape[0], dtype=jnp.int32) % head_count
+    owners = requests // block_count
+    offsets = requests % block_count
+    one_hot = (owners[:, None] == jnp.arange(seq_count, dtype=jnp.int32)[None, :]).astype(jnp.int32)
+    position = jnp.sum(one_hot * (jnp.cumsum(one_hot, axis=0) - 1), axis=1)
+    return owners, position, offsets * head_count + head_of
 
 
 def per_device(queries, key_rows, values, rand_blocks, out_weight, cotangent):
@@ -66,22 +86,20 @@
     key_value = jnp.concatenate([stacked[1], stacked[2]], axis=1)
     padded = with_halo(key_value, (("seq", 0),), block_len)
     first_block = broadcast_first(key_value[:block_len], "seq")
-    requests = jnp.transpose(rand_blocks, (0, 2, 1)).reshape(-1)
-    request_count = requests.shape[0]
-    head_of = jnp.arange(request_count, dtype=jnp.int32) % head_count
+    request_count = rand_blocks.shape[0] * rand_blocks.shape[1] * rand_blocks.shape[2]
     capacity = 3 * request_count // (2 * seq_count)
-    owners = requests // block_count
-    offsets = requests % block_count
-    one_hot = (owners[:, None] == jnp.arange(seq_count, dtype=jnp.int32)[None, :]).astype(jnp.int32)
-    position = jnp.sum(one_hot * (jnp.cumsum(one_hot, axis=0) - 1), axis=1)
+    owners, position, codes = request_slots(
+        rand_blocks, block_count, head_count, seq_count, capacity
+    )
     slot_of = owners * capacity + position
-    asked_codes = (
-        jnp.full((seq_count * capacity,), -1, jnp.int32)
-        .at[slot_of]
-        .set(offsets * head_count + head_of)
-        .reshape(seq_count, capacity)
-    )
-    asked_here = lax.all_to_all(asked_codes, "seq", split_axis=0, concat_axis=0, tiled=True)
+    every_block = lax.all_gather(rand_blocks, "seq", axis=0, tiled=False)
+    all_owners, all_position, all_codes = jax.vmap(
+        lambda r: request_slots(r, block_count, head_count, seq_count, capacity)
+    )(every_block)
+    match = (all_owners[:, :, None] == seq_index) & (
+        all_position[:, :, None] == jnp.arange(capacity, dtype=jnp.int32)[None, None, :]
+    )
+    asked_here = jnp.sum(jnp.where(match, all_codes[:, :, None] + 1, 0), axis=1) - 1
     slot_total = seq_count * capacity
     pair_count = block_count * head_count
     asked_flat = asked_here.reshape(slot_total)
@@ -303,12 +321,17 @@
     grad_k = core[:, :, 0].reshape(shard_len, width_cols).astype(jnp.bfloat16)
     grad_v = core[:, :, 1].reshape(shard_len, width_cols).astype(jnp.bfloat16)
     grad_q_rows = grad_q.reshape(shard_len, width_cols)
-    back = jnp.stack([grad_q_rows, grad_k, grad_v]).reshape(3, group_count, piece_len, width_cols)
-    back = lax.all_to_all(
-        jnp.transpose(back, (1, 0, 2, 3)), "head", split_axis=0, concat_axis=0, tiled=True
-    )
-    back = jnp.transpose(back, (1, 2, 0, 3)).reshape(3, 1, piece_len, group_count * width_cols)
-    grad_queries, grad_keys, grad_values = back[0], back[1], back[2]
+    def to_owners(rows):
+        count = rows.shape[0]
+        rows = rows.reshape(count, group_count, piece_len, width_cols)
+        rows = lax.all_to_all(
+            jnp.transpose(rows, (1, 0, 2, 3)), "head", split_axis=0, concat_axis=0, tiled=True
+        )
+        return jnp.transpose(rows, (1, 2, 0, 3)).reshape(count, 1, piece_len, group_count * width_cols)
+
+    grad_queries = to_owners(grad_q_rows[None])[0]
+    back = to_owners(jnp.stack([grad_k, grad_v]))
+    grad_keys, grad_values = back[0], back[1]
     return (layer_out, grad_queries, grad_keys, grad_values, weight_grad)
 
 

time: 548 us -> 531 us (0.969)
  waiting for transfers between devices: 203 us -> 156 us
  other arithmetic: 56.1 us -> 71.3 us
  starting transfers between devices: 69.8 us -> 79.2 us
  blocking collectives: 15.1 us -> 22.3 us
    all_to_all x1, waiting for transfers between devices: 22.4 us -> 0.01 us  [per_device(): lax.all_to_all(stacked, 'head', split_axis=0, concat_axis=0, tiled=True)]
    all_gather x0 -> x1, blocking collectives: none -> 22.3 us  [per_device(): every_block = lax.all_gather(rand_blocks, 'seq', axis=0, tiled=False)]
    ppermute x4 -> x6, waiting for transfers between devices: 55.6 us -> 39.7 us  [reduce_to_first(): total = total + lax.ppermute(block, axis, pairs)]
    all_to_all x1 -> x0, blocking collectives: 15.1 us -> none  [per_device(): lax.all_to_all(asked_codes, 'seq', split_axis=0, concat_axis=0, tiled=True)]
    all_to_all x2, waiting for transfers between devices: 40.4 us -> 26.5 us  [fetch(): lax.all_to_all(served, 'seq', split_axis=0, concat_axis=0, tiled=True)]
    another operation x6 -> x10, other arithmetic: 5.17 us -> 14.3 us
    ppermute x4 -> x6, waiting for transfers between devices: 29.8 us -> 27.3 us  [broadcast_first(): got = lax.ppermute(block, axis, pairs)]
    ppermute x4 -> x6, starting transfers between devices: 12.3 us -> 14.6 us  [broadcast_first(): got = lax.ppermute(block, axis, pairs)]
  transfers between devices with their start and end apart: 23 -> 28, of which waited for: 9 -> 8; matrix products, arithmetic and copies ran while one was open for 33% -> 37% of each run, Pallas kernels for 0% -> 0%
where the time goes in v4:
time: 531 us; the launch traced here: 521 us
  waiting for transfers between devices  156 us (29%)
  local copies, waits for them, and re-layouts  106 us (20%)
  starting transfers between devices  79.2 us (15%)
  matrix products  71.8 us (14%)
  other arithmetic  71.3 us (13%)
  blocking collectives  22.3 us (4%)
  between operations  15.2 us (3%)
    ppermute x6, waiting for transfers between devices, reduce_to_first(): total = total + lax.ppermute(block, axis, pairs)  39.7 us
    all_to_all x2, waiting for transfers between devices, to_owners(): lax.all_to_all(jnp.transpose(rows, (1, 0, 2, 3)), 'head', split_axis=0, c...  36.8 us
    unnamed x89, local copies, waits for them, and re-layouts  29.1 us
    ppermute x6, waiting for transfers between devices, broadcast_first(): got = lax.ppermute(block, axis, pairs)  27.3 us
    all_to_all x2, waiting for transfers between devices, fetch(): lax.all_to_all(served, 'seq', split_axis=0, concat_axis=0, tiled=True)  26.5 us
    all_gather x1, blocking collectives, per_device(): every_block = lax.all_gather(rand_blocks, 'seq', axis=0, tiled=False)  22.3 us
    all_to_all x2, waiting for transfers between devices, give_back(): lax.all_to_all(outgoing, 'seq', split_axis=0, concat_axis=0, tiled=True)  20.9 us
    ppermute x6, starting transfers between devices, broadcast_first(): got = lax.ppermute(block, axis, pairs)  14.6 us
  transfers between devices with their start and end apart: 28, of which 8 were waited for; matrix products, arithmetic and copies ran while one was open for 37% of the time, Pallas kernels for 0%

profile of v4, /device:TPU:1, one launch (start us, length us, event | category | flops | bytes accessed | tf_op | source)
XLA Modules:
  0.0 521.3 jit_solution(17961939478082555063)
XLA Ops:
  10.3 5.3 %reshape.611 = bf16[3,160,4,512]{3,2,1,0:T(4,128)(2,1)} reshape(bf16[3,160,2048]{2,1,0:T(8,128)(2,1)} %pad_maximum_fusion.1) | data formatting | bytes 3932160 | tf_op jit(solution)/shard_map/reshape | solution.py:78
  18.8 5.1 all-to-all-start
  24.0 22.3 %all-gather = s32[160,4,4]{2,1,0:T(4,128)S(1)} all-gather(s32[10,4,4]{2,1,0:T(4,128)S(1)} %copy.420), channel_id=2, replica_groups=mesh['dp'=2,'seq'=16,'head'=4] {'seq'}, dimensions={0}, use_global_device_ids=true | all-gather | bytes 10880 | tf_op jit(solution)/shard_map/all_gather | solution.py:95
  47.8 9.1 %reduce-window.16 = s32[16,16,2,128]{3,1,2,0:T(8,128)S(1)} reduce-window(s32[16,16,2,128]{3,1,2,0:T(8,128)S(1)} %copy_bitcast_fusion.2, s32[]{:T(128)} %constant.262.clone.1), window={size=1x1x1x128 pad=0_0x0_0x0_0x127_0}, to_apply=%region_5.6 | reduce-window | flops 8323072 | bytes 524292 | tf_op jit(solution)/shard_map/reduce-window.2
  70.5 4.9 pad_maximum_fusion.5
  83.1 8.0 %all-to-all-start.1 = ((bf16[16,15,64,128]{3,2,1,0:T(8,128)(2,1)}), bf16[16,15,64,128]{3,2,1,0:T(8,128)(2,1)}, u32[]{:S(2)}, u32[]{:S(2)}) async-start(bf16[16,15,64,128]{3,2,1,0:T(8,128)(2,1)} %bitcast.342), calls=%async_computation.1 | async-start | bytes 7864320 | tf_op jit(solution)/shard_map/all_to_all | solution.py:119
  93.7 5.1 collective-permute-start.2
  108.1 27.3 %collective-permute-done.2 = bf16[64,1024]{1,0:T(8,128)(2,1)} collective-permute-done((bf16[64,1024]{1,0:T(8,128)(2,1)S(1)}, bf16[64,1024]{1,0:T(8,128)(2,1)}, u32[]{:S(2)}, u32[]{:S(2)}) %collective-permute-start.2) | collective-permute-done | bytes 131104 | tf_op jit(solution)/shard_map/ppermute | solution.py:37
  149.3 4.9 pad_maximum_fusion
  161.7 5.8 %all-to-all-start.2 = ((bf16[16,15,64,128]{3,2,1,0:T(8,128)(2,1)}), bf16[16,15,64,128]{3,2,1,0:T(8,128)(2,1)}, u32[]{:S(2)}, u32[]{:S(2)}) async-start(bf16[16,15,64,128]{3,2,1,0:T(8,128)(2,1)} %bitcast.344), calls=%async_computation.2 | async-start | bytes 7864320 | tf_op jit(solution)/shard_map/all_to_all | solution.py:119
  167.6 5.1 select_reduce_fusion
  182.2 4.8 fusion.52
  197.3 26.5 %all-to-all-done.2 = bf16[16,15,64,128]{3,2,1,0:T(8,128)(2,1)} async-done(((bf16[16,15,64,128]{3,2,1,0:T(8,128)(2,1)}), bf16[16,15,64,128]{3,2,1,0:T(8,128)(2,1)}, u32[]{:S(2)}, u32[]{:S(2)}) %all-to-all-start.2) | async-done | bytes 3932192 | tf_op jit(solution)/shard_map/all_to_all | solution.py:119
  223.7 4.8 fusion.55
  272.6 7.5 %all-to-all-start.5 = ((bf16[16,15,64,128]{3,2,1,0:T(8,128)(2,1)}), bf16[16,15,64,128]{3,2,1,0:T(8,128)(2,1)}, u32[]{:S(2)}, u32[]{:S(2)}) async-start(bf16[16,15,64,128]{3,2,1,0:T(8,128)(2,1)} %bitcast.345), calls=%async_computation.6 | async-start | bytes 7864320 | tf_op jit(solution)/shard_map/all_to_all | solution.py:312
  280.5 5.0 multiply_convert_fusion.1
  322.5 20.9 %all-to-all-done.5 = bf16[16,15,64,128]{3,2,1,0:T(8,128)(2,1)} async-done(((bf16[16,15,64,128]{3,2,1,0:T(8,128)(2,1)}), bf16[16,15,64,128]{3,2,1,0:T(8,128)(2,1)}, u32[]{:S(2)}, u32[]{:S(2)}) %all-to-all-start.5) | async-done | bytes 3932192 | tf_op jit(solution)/shard_map/all_to_all | solution.py:312
  348.2 4.8 fusion.19
  361.7 39.6 %collective-permute-done.13 = f32[64,1024]{1,0:T(8,128)S(1)} collective-permute-done((f32[64,1024]{1,0:T(8,128)S(1)}, f32[64,1024]{1,0:T(8,128)S(1)}, u32[]{:S(2)}, u32[]{:S(2)}) %collective-permute-start.13) | collective-permute-done | bytes 262176 | tf_op jit(solution)/shard_map/ppermute | solution.py:53
  433.5 5.9 %fusion.59 = f32[10,4,64,1,128]{4,0,2,1,3:T(8,128)} fusion(s32[10,4]{0,1:T(4,128)S(1)} %multiply_add_fusion, s32[240]{0:T(256)S(1)} %sub.106, bf16[30,8,64,128]{3,2,1,0:T(8,128)(2,1)} %bitcast.158), kind=kOutput, calls=%fused_computation.88 | convolution fusion | flops 157296000 | bytes 5244000 | tf_op jit(solution)/shard_map/dot_general | solution.py:313
  451.4 4.8 fusion.58
  461.1 8.8 %all-to-all-done.3 = bf16[4,1,160,512]{3,2,1,0:T(8,128)(2,1)} async-done(((bf16[4,1,160,512]{3,2,1,0:T(8,128)(2,1)}), bf16[4,1,160,512]{3,2,1,0:T(8,128)(2,1)}, u32[]{:S(2)}, u32[]{:S(2)}) %all-to-all-start.3) | async-done | bytes 655392 | tf_op jit(solution)/shard_map/all_to_all | solution.py:327
  475.4 28.0 %all-to-all-done.6 = bf16[4,2,160,512]{3,2,1,0:T(8,128)(2,1)S(1)} async-done(((bf16[4,2,160,512]{3,2,1,0:T(8,128)(2,1)}), bf16[4,2,160,512]{3,2,1,0:T(8,128)(2,1)S(1)}, u32[]{:S(2)}, u32[]{:S(2)}) %all-to-all-start.6) | async-done | bytes 1310752 | tf_op jit(solution)/shard_map/all_to_all | solution.py:327
  505.3 6.7 %maximum_select_fusion = f32[512,2048]{1,0:T(8,128)} fusion(f32[256,2048]{1,0:T(8,128)} %collective-permute-done.17, f32[256,2048]{1,0:T(8,128)} %broadcast_multiply_fusion, pred[]{:T(512)S(6)} %eq.186), kind=kLoop, calls=%fused_computation.16 | loop fusion | flops 3145728 | bytes 8388609 | tf_op jit(solution)/shard_map/jit(_where)/select_n | solution.py:207
  (283 shorter events, 235.0 us)
Async XLA Ops:
  18.8 39.2 %all-to-all-start = ((bf16[4,3,160,512]{3,2,1,0:T(8,128)(2,1)}), bf16[4,3,160,512]{3,2,1,0:T(8,128)(2,1)}, u32[]{:S(2)}, u32[]{:S(2)}) async-start(bf16[4,3,160,512]{3,2,1,0:T(8,128)(2,1)} %copy.409), calls=%async_computation | async-start | bytes 3932160 | tf_op jit(solution)/shard_map/all_to_all | solution.py:79
  83.1 78.6 %all-to-all-start.1 = ((bf16[16,15,64,128]{3,2,1,0:T(8,128)(2,1)}), bf16[16,15,64,128]{3,2,1,0:T(8,128)(2,1)}, u32[]{:S(2)}, u32[]{:S(2)}) async-start(bf16[16,15,64,128]{3,2,1,0:T(8,128)(2,1)} %bitcast.342), calls=%async_computation.1 | async-start | bytes 7864320 | tf_op jit(solution)/shard_map/all_to_all | solution.py:119
  91.1 85.1 %all-gather.3.cloned.1.call-start = ((), (), s32[]{:S(2)}) async-start(), calls=%async_computation.9 | async-start | bytes 3276800 | tf_op jit(solution)/shard_map/all_gather | solution.py:194
  93.7 41.7 %collective-permute-start.2 = (bf16[64,1024]{1,0:T(8,128)(2,1)S(1)}, bf16[64,1024]{1,0:T(8,128)(2,1)}, u32[]{:S(2)}, u32[]{:S(2)}) collective-permute-start(bf16[64,1024]{1,0:T(8,128)(2,1)S(1)} %get-tuple-element.104), channel_id=1, source_target_pairs={{0,48},{1,49},{2,50},{3,51},{64,112},{65,113},{66,114},{67,115}} | collective-permute-start | bytes 393224 | tf_op jit(solution)/shard_map/ppermute | solution.py:37
  98.8 36.6 %collective-permute-start.3 = (bf16[64,1024]{1,0:T(8,128)(2,1)S(1)}, bf16[64,1024]{1,0:T(8,128)(2,1)}, u32[]{:S(2)}, u32[]{:S(2)}) collective-permute-start(bf16[64,1024]{1,0:T(8,128)(2,1)S(1)} %get-tuple-element.104), channel_id=1, source_target_pairs={{0,32},{1,33},{2,34},{3,35},{64,96},{65,97},{66,98},{67,99}} | collective-permute-start | bytes 393224 | tf_op jit(solution)/shard_map/ppermute | solution.py:37
  100.7 34.7 %collective-permute-start.4 = (bf16[64,1024]{1,0:T(8,128)(2,1)S(1)}, bf16[64,1024]{1,0:T(8,128)(2,1)}, u32[]{:S(2)}, u32[]{:S(2)}) collective-permute-start(bf16[64,1024]{1,0:T(8,128)(2,1)S(1)} %get-tuple-element.104), channel_id=1, source_target_pairs={{0,16},{1,17},{2,18},{3,19},{64,80},{65,81},{66,82},{67,83}} | collective-permute-start | bytes 393224 | tf_op jit(solution)/shard_map/ppermute | solution.py:37
  136.1 36.6 %collective-permute-start.5 = (bf16[64,1024]{1,0:T(8,128)(2,1)}, bf16[64,1024]{1,0:T(8,128)(2,1)S(1)}, u32[]{:S(2)}, u32[]{:S(2)}) collective-permute-start(bf16[64,1024]{1,0:T(8,128)(2,1)} %select_select_fusion.1), channel_id=1, source_target_pairs={{0,12},{16,28},{32,44},{48,60},{1,13},{17,29},{33,45},{49,61},{2,1... | collective-permute-start | bytes 393224 | tf_op jit(solution)/shard_map/ppermute | solution.py:37
  137.4 35.3 %collective-permute-start.6 = (bf16[64,1024]{1,0:T(8,128)(2,1)}, bf16[64,1024]{1,0:T(8,128)(2,1)}, u32[]{:S(2)}, u32[]{:S(2)}) collective-permute-start(bf16[64,1024]{1,0:T(8,128)(2,1)} %select_select_fusion.1), channel_id=1, source_target_pairs={{0,8},{16,24},{32,40},{48,56},{1,9},{17,25},{33,41},{49,57},{2,10}... | collective-permute-start | bytes 393224 | tf_op jit(solution)/shard_map/ppermute | solution.py:37
  139.4 33.4 %collective-permute-start.7 = (bf16[64,1024]{1,0:T(8,128)(2,1)}, bf16[64,1024]{1,0:T(8,128)(2,1)}, u32[]{:S(2)}, u32[]{:S(2)}) collective-permute-start(bf16[64,1024]{1,0:T(8,128)(2,1)} %select_select_fusion.1), channel_id=1, source_target_pairs={{0,4},{16,20},{32,36},{48,52},{1,5},{17,21},{33,37},{49,53},{2,6},... | collective-permute-start | bytes 393224 | tf_op jit(solution)/shard_map/ppermute | solution.py:37
  161.7 62.0 %all-to-all-start.2 = ((bf16[16,15,64,128]{3,2,1,0:T(8,128)(2,1)}), bf16[16,15,64,128]{3,2,1,0:T(8,128)(2,1)}, u32[]{:S(2)}, u32[]{:S(2)}) async-start(bf16[16,15,64,128]{3,2,1,0:T(8,128)(2,1)} %bitcast.344), calls=%async_computation.2 | async-start | bytes 7864320 | tf_op jit(solution)/shard_map/all_to_all | solution.py:119
  167.6 271.8 %all-reduce.5.cloned.1.call-start = ((), (), s32[]{:S(2)}) async-start(), calls=%async_computation.10 | async-start | bytes 4194304 | tf_op jit(solution)/shard_map/psum | solution.py:205
  249.7 105.4 %collective-permute-start.10 = (f32[64,1024]{1,0:T(8,128)}, f32[64,1024]{1,0:T(8,128)}, u32[]{:S(2)}, u32[]{:S(2)}) collective-permute-start(f32[64,1024]{1,0:T(8,128)} %reshape.629), channel_id=1, source_target_pairs={{12,0},{28,16},{44,32},{60,48},{13,1},{29,17},{45,33},{61,49},{14,... | collective-permute-start | bytes 786440 | tf_op jit(solution)/shard_map/ppermute | solution.py:53
  251.0 104.1 %collective-permute-start.9 = (f32[64,1024]{1,0:T(8,128)}, f32[64,1024]{1,0:T(8,128)}, u32[]{:S(2)}, u32[]{:S(2)}) collective-permute-start(f32[64,1024]{1,0:T(8,128)} %reshape.629), channel_id=1, source_target_pairs={{8,0},{24,16},{40,32},{56,48},{9,1},{25,17},{41,33},{57,49},{10,2}... | collective-permute-start | bytes 786440 | tf_op jit(solution)/shard_map/ppermute | solution.py:53
  252.3 102.8 %collective-permute-start.8 = (f32[64,1024]{1,0:T(8,128)}, f32[64,1024]{1,0:T(8,128)}, u32[]{:S(2)}, u32[]{:S(2)}) collective-permute-start(f32[64,1024]{1,0:T(8,128)} %reshape.629), channel_id=1, source_target_pairs={{4,0},{20,16},{36,32},{52,48},{5,1},{21,17},{37,33},{53,49},{6,2},... | collective-permute-start | bytes 786440 | tf_op jit(solution)/shard_map/ppermute | solution.py:53
  272.6 70.8 %all-to-all-start.5 = ((bf16[16,15,64,128]{3,2,1,0:T(8,128)(2,1)}), bf16[16,15,64,128]{3,2,1,0:T(8,128)(2,1)}, u32[]{:S(2)}, u32[]{:S(2)}) async-start(bf16[16,15,64,128]{3,2,1,0:T(8,128)(2,1)} %bitcast.345), calls=%async_computation.6 | async-start | bytes 7864320 | tf_op jit(solution)/shard_map/all_to_all | solution.py:312
  280.1 232.0 %reduce-scatter.2.cloned.1.call-start = ((), (), s32[]{:S(2)}) async-start(), calls=%async_computation.8 | async-start | bytes 6553600 | tf_op jit(solution)/shard_map/reduce_scatter | solution.py:188
  343.4 103.6 %all-to-all-start.4 = ((bf16[16,15,64,128]{3,2,1,0:T(8,128)(2,1)}), bf16[16,15,64,128]{3,2,1,0:T(8,128)(2,1)}, u32[]{:S(2)}, u32[]{:S(2)}) async-start(bf16[16,15,64,128]{3,2,1,0:T(8,128)(2,1)} %bitcast.343), calls=%async_computation.5 | async-start | bytes 7864320 | tf_op jit(solution)/shard_map/all_to_all | solution.py:312
  356.3 45.1 %collective-permute-start.13 = (f32[64,1024]{1,0:T(8,128)S(1)}, f32[64,1024]{1,0:T(8,128)S(1)}, u32[]{:S(2)}, u32[]{:S(2)}) collective-permute-start(f32[64,1024]{1,0:T(8,128)S(1)} %add_add_fusion), channel_id=1, source_target_pairs={{48,0},{49,1},{50,2},{51,3},{112,64},{113,65},{114,66},{115,67}} | collective-permute-start | bytes 786440 | tf_op jit(solution)/shard_map/ppermute | solution.py:53
  357.6 43.8 %collective-permute-start.12 = (f32[64,1024]{1,0:T(8,128)S(1)}, f32[64,1024]{1,0:T(8,128)S(1)}, u32[]{:S(2)}, u32[]{:S(2)}) collective-permute-start(f32[64,1024]{1,0:T(8,128)S(1)} %add_add_fusion), channel_id=1, source_target_pairs={{32,0},{33,1},{34,2},{35,3},{96,64},{97,65},{98,66},{99,67}} | collective-permute-start | bytes 786440 | tf_op jit(solution)/shard_map/ppermute | solution.py:53
  358.9 42.5 %collective-permute-start.11 = (f32[64,1024]{1,0:T(8,128)S(1)}, f32[64,1024]{1,0:T(8,128)S(1)}, u32[]{:S(2)}, u32[]{:S(2)}) collective-permute-start(f32[64,1024]{1,0:T(8,128)S(1)} %add_add_fusion), channel_id=1, source_target_pairs={{16,0},{17,1},{18,2},{19,3},{80,64},{81,65},{82,66},{83,67}} | collective-permute-start | bytes 786440 | tf_op jit(solution)/shard_map/ppermute | solution.py:53
  406.9 19.1 %collective-permute-start.15 = (bf16[64,1024]{1,0:T(8,128)(2,1)S(1)}, bf16[64,1024]{1,0:T(8,128)(2,1)}, u32[]{:S(2)}, u32[]{:S(2)}) collective-permute-start(bf16[64,1024]{1,0:T(8,128)(2,1)S(1)} %concatenate.48), channel_id=1, source_target_pairs={{4,0},{8,4},{12,8},{16,12},{20,16},{24,20},{28,24},{32,28},{36,32}... | collective-permute-start | bytes 393224 | tf_op jit(solution)/shard_map/ppermute | solution.py:20
  442.6 62.8 %collective-permute-start.17 = (f32[256,2048]{1,0:T(8,128)}, f32[256,2048]{1,0:T(8,128)}, u32[]{:S(2)}, u32[]{:S(2)}) collective-permute-start(f32[256,2048]{1,0:T(8,128)} %broadcast_multiply_fusion), channel_id=1, source_target_pairs={{0,64},{64,0},{1,65},{65,1},{2,66},{66,2},{3,67},{67,3},{4,68},{68... | collective-permute-start | bytes 6291464 | tf_op jit(solution)/shard_map/ppermute | solution.py:206
  447.0 22.9 %all-to-all-start.3 = ((bf16[4,1,160,512]{3,2,1,0:T(8,128)(2,1)}), bf16[4,1,160,512]{3,2,1,0:T(8,128)(2,1)}, u32[]{:S(2)}, u32[]{:S(2)}) async-start(bf16[4,1,160,512]{3,2,1,0:T(8,128)(2,1)} %bitcast.43), calls=%async_computation.4 | async-start | bytes 1310720 | tf_op jit(solution)/shard_map/all_to_all | solution.py:327
  469.9 33.6 %all-to-all-start.6 = ((bf16[4,2,160,512]{3,2,1,0:T(8,128)(2,1)}), bf16[4,2,160,512]{3,2,1,0:T(8,128)(2,1)S(1)}, u32[]{:S(2)}, u32[]{:S(2)}) async-start(bf16[4,2,160,512]{3,2,1,0:T(8,128)(2,1)} %copy.488), calls=%async_computation.7 | async-start | bytes 2621440 | tf_op jit(solution)/shard_map/all_to_all | solution.py:327
  (44 other events, 349.1 us)
Sparse Core Ops, SparseCore 0:
  93.6 41.8 all-gather.2
  263.7 161.0 all-reduce.4
  427.2 74.3 reduce-scatter.1

commit v5 on v4

--- a/solution.py
+++ b/solution.py
@@ -185,12 +185,18 @@
     attn = (mixed / totals_rows).astype(jnp.bfloat16)
     logsum = row_max + jnp.log(totals)
     attn_rows = attn.reshape(shard_len, width_cols)
-    layer_out = lax.psum_scatter(
-        jnp.dot(attn_rows, out_weight, preferred_element_type=jnp.float32),
-        "head",
-        scatter_dimension=0,
-        tiled=True,
-    ).astype(jnp.bfloat16)[None]
+    head_index = lax.axis_index("head")
+    out_parts = jnp.dot(attn_rows, out_weight, preferred_element_type=jnp.float32).reshape(
+        group_count, piece_len, -1
+    )
+    out_sum = lax.dynamic_index_in_dim(out_parts, head_index, axis=0, keepdims=False)
+    for shift in range(1, group_count):
+        pairs = [(i, (i + shift) % group_count) for i in range(group_count)]
+        sent = lax.dynamic_index_in_dim(
+            out_parts, (head_index + shift) % group_count, axis=0, keepdims=False
+        )
+        out_sum = out_sum + lax.ppermute(sent, "head", pairs)
+    layer_out = out_sum.astype(jnp.bfloat16)[None]
     piece_flat = lax.all_gather(cotangent, "head", axis=1, tiled=True)[0]
     grad_piece = jnp.dot(piece_flat, out_weight.T, preferred_element_type=jnp.float32).astype(
         jnp.bfloat16

time: 531 us -> 558 us (1.051)
  starting transfers between devices: 79.2 us -> 96.9 us
  local copies, waits for them, and re-layouts: 106 us -> 115 us
    psum x1, waiting for transfers between devices: 0.01 us -> 33.4 us  [per_device(): mine = lax.psum(mine, 'seq') * (1.0 / math.sqrt(token_total))]
    all_to_all x2, waiting for transfers between devices: 36.8 us -> 11.6 us  [to_owners(): lax.all_to_all(jnp.transpose(rows, (1, 0, 2, 3)), 'head', split_axis=0, c...]
    all_to_all x2, waiting for transfers between devices: 20.9 us -> 0.57 us  [give_back(): lax.all_to_all(outgoing, 'seq', split_axis=0, concat_axis=0, tiled=True)]
    all_to_all x2, waiting for transfers between devices: 26.5 us -> 38.4 us  [fetch(): lax.all_to_all(served, 'seq', split_axis=0, concat_axis=0, tiled=True)]
    ppermute x0 -> x3, starting transfers between devices: none -> 8.2 us  [per_device(): out_sum = out_sum + lax.ppermute(sent, 'head', pairs)]
    all_to_all x2, starting transfers between devices: 12.2 us -> 19.2 us  [give_back(): lax.all_to_all(outgoing, 'seq', split_axis=0, concat_axis=0, tiled=True)]
    unnamed x89 -> x75, local copies, waits for them, and re-layouts: 29.1 us -> 30.1 us
  transfers between devices with their start and end apart: 28 -> 30, of which waited for: 8 -> 9; matrix products, arithmetic and copies ran while one was open for 37% -> 34% of each run, Pallas kernels for 0% -> 0%
where the time goes in v5:
time: 558 us; the launch traced here: 547 us
  waiting for transfers between devices  158 us (28%)
  local copies, waits for them, and re-layouts  115 us (21%)
  starting transfers between devices  96.9 us (17%)
  matrix products  70.8 us (13%)
  other arithmetic  68.6 us (12%)
  blocking collectives  22.3 us (4%)
  between operations  15.5 us (3%)
    all_to_all x2, waiting for transfers between devices, fetch(): lax.all_to_all(served, 'seq', split_axis=0, concat_axis=0, tiled=True)  38.4 us
    ppermute x6, waiting for transfers between devices, reduce_to_first(): total = total + lax.ppermute(block, axis, pairs)  37.7 us
    psum x1, waiting for transfers between devices, per_device(): mine = lax.psum(mine, 'seq') * (1.0 / math.sqrt(token_total))  33.4 us
    ppermute x6, waiting for transfers between devices, broadcast_first(): got = lax.ppermute(block, axis, pairs)  32.1 us
    unnamed x75, local copies, waits for them, and re-layouts  30.1 us
    all_gather x1, blocking collectives, per_device(): every_block = lax.all_gather(rand_blocks, 'seq', axis=0, tiled=False)  22.3 us
    all_to_all x2, starting transfers between devices, give_back(): lax.all_to_all(outgoing, 'seq', split_axis=0, concat_axis=0, tiled=True)  19.2 us
    all_to_all x2, starting transfers between devices, fetch(): lax.all_to_all(served, 'seq', split_axis=0, concat_axis=0, tiled=True)  18.8 us
  transfers between devices with their start and end apart: 30, of which 9 were waited for; matrix products, arithmetic and copies ran while one was open for 34% of the time, Pallas kernels for 0%

profile of v5, /device:TPU:1, one launch (start us, length us, event | category | flops | bytes accessed | tf_op | source)
XLA Modules:
  0.0 547.3 jit_solution(13663801751060278435)
XLA Ops:
  10.3 5.3 reshape.614
  18.8 5.1 all-to-all-start
  24.0 22.3 %all-gather = s32[160,4,4]{2,1,0:T(4,128)S(1)} all-gather(s32[10,4,4]{2,1,0:T(4,128)S(1)} %copy.425), channel_id=2, replica_groups=mesh['dp'=2,'seq'=16,'head'=4] {'seq'}, dimensions={0}, use_global_device_ids=true | all-gather | bytes 10880 | tf_op jit(solution)/shard_map/all_gather | solution.py:95
  47.8 9.1 %reduce-window.16 = s32[16,16,2,128]{3,1,2,0:T(8,128)S(1)} reduce-window(s32[16,16,2,128]{3,1,2,0:T(8,128)S(1)} %copy_bitcast_fusion.2, s32[]{:T(128)} %constant.286.clone.1), window={size=1x1x1x128 pad=0_0x0_0x0_0x127_0}, to_apply=%region_5.6 | reduce-window | flops 8323072 | bytes 524292 | tf_op jit(solution)/shard_map/reduce-window.2
  70.4 4.9 pad_maximum_fusion.5
  83.1 8.0 %all-to-all-start.1 = ((bf16[16,15,64,128]{3,2,1,0:T(8,128)(2,1)}), bf16[16,15,64,128]{3,2,1,0:T(8,128)(2,1)}, u32[]{:S(2)}, u32[]{:S(2)}) async-start(bf16[16,15,64,128]{3,2,1,0:T(8,128)(2,1)} %bitcast.361), calls=%async_computation.1 | async-start | bytes 7864320 | tf_op jit(solution)/shard_map/all_to_all | solution.py:119
  97.7 38.4 %all-to-all-done.1 = bf16[16,15,64,128]{3,2,1,0:T(8,128)(2,1)} async-done(((bf16[16,15,64,128]{3,2,1,0:T(8,128)(2,1)}), bf16[16,15,64,128]{3,2,1,0:T(8,128)(2,1)}, u32[]{:S(2)}, u32[]{:S(2)}) %all-to-all-start.1) | async-done | bytes 3932192 | tf_op jit(solution)/shard_map/all_to_all | solution.py:119
  136.0 10.8 %all-to-all-start.2 = ((bf16[16,15,64,128]{3,2,1,0:T(8,128)(2,1)}), bf16[16,15,64,128]{3,2,1,0:T(8,128)(2,1)}, u32[]{:S(2)}, u32[]{:S(2)}) async-start(bf16[16,15,64,128]{3,2,1,0:T(8,128)(2,1)} %bitcast.356), calls=%async_computation.2 | async-start | bytes 7864320 | tf_op jit(solution)/shard_map/all_to_all | solution.py:119
  156.0 29.0 %collective-permute-done.4 = bf16[64,1024]{1,0:T(8,128)(2,1)} collective-permute-done((bf16[64,1024]{1,0:T(8,128)(2,1)S(1)}, bf16[64,1024]{1,0:T(8,128)(2,1)}, u32[]{:S(2)}, u32[]{:S(2)}) %collective-permute-start.4) | collective-permute-done | bytes 131104 | tf_op jit(solution)/shard_map/ppermute | solution.py:37
  203.9 4.9 pad_maximum_fusion
  224.5 4.8 fusion.54
  231.6 4.8 fusion.57
  261.2 5.0 multiply_convert_fusion.1
  284.5 10.6 %all-to-all-start.5 = ((bf16[16,15,64,128]{3,2,1,0:T(8,128)(2,1)}), bf16[16,15,64,128]{3,2,1,0:T(8,128)(2,1)}, u32[]{:S(2)}, u32[]{:S(2)}) async-start(bf16[16,15,64,128]{3,2,1,0:T(8,128)(2,1)} %bitcast.362), calls=%async_computation.5 | async-start | bytes 7864320 | tf_op jit(solution)/shard_map/all_to_all | solution.py:318
  300.5 4.7 collective-permute-start.19
  342.7 8.6 %all-to-all-start.4 = ((bf16[16,15,64,128]{3,2,1,0:T(8,128)(2,1)}), bf16[16,15,64,128]{3,2,1,0:T(8,128)(2,1)}, u32[]{:S(2)}, u32[]{:S(2)}) async-start(bf16[16,15,64,128]{3,2,1,0:T(8,128)(2,1)} %bitcast.357), calls=%async_computation.4 | async-start | bytes 7864320 | tf_op jit(solution)/shard_map/all_to_all | solution.py:318
  367.8 37.7 %collective-permute-done.16 = f32[64,1024]{1,0:T(8,128)} collective-permute-done((f32[64,1024]{1,0:T(8,128)}, f32[64,1024]{1,0:T(8,128)}, u32[]{:S(2)}, u32[]{:S(2)}) %collective-permute-start.16) | collective-permute-done | bytes 262176 | tf_op jit(solution)/shard_map/ppermute | solution.py:53
  445.4 5.9 %fusion.61 = f32[10,4,64,1,128]{4,0,2,1,3:T(8,128)} fusion(s32[10,4]{0,1:T(4,128)S(1)} %multiply_add_fusion, s32[240]{0:T(256)S(1)} %sub.106, bf16[30,8,64,128]{3,2,1,0:T(8,128)(2,1)} %bitcast.160), kind=kOutput, calls=%fused_computation.90 | convolution fusion | flops 157296000 | bytes 5244000 | tf_op jit(solution)/shard_map/dot_general | solution.py:319
  451.3 33.4 %all-reduce.5.cloned.1.call-done = f32[256,2048]{1,0:T(8,128)} async-done(((f32[256,2048]{1,0:T(8,128)}), f32[256,2048]{1,0:T(8,128)}) %all-reduce.5.cloned.1.call-update) | async-done | bytes 2097168 | tf_op jit(solution)/shard_map/psum | solution.py:211
  489.9 4.4 all-to-all-start.3
  494.3 4.7 fusion.60
  510.0 4.2 all-to-all-start.6
  519.9 11.6 %all-to-all-done.6 = bf16[4,2,160,512]{3,2,1,0:T(8,128)(2,1)S(1)} async-done(((bf16[4,2,160,512]{3,2,1,0:T(8,128)(2,1)}), bf16[4,2,160,512]{3,2,1,0:T(8,128)(2,1)S(1)}, u32[]{:S(2)}, u32[]{:S(2)}) %all-to-all-start.6) | async-done | bytes 1310752 | tf_op jit(solution)/shard_map/all_to_all | solution.py:333
  533.4 6.6 %maximum_select_fusion = f32[512,2048]{1,0:T(8,128)} fusion(f32[256,2048]{1,0:T(8,128)} %collective-permute-done.20, f32[256,2048]{1,0:T(8,128)} %broadcast_multiply_fusion, pred[]{:T(512)S(6)} %eq.189), kind=kLoop, calls=%fused_computation.16 | loop fusion | flops 3145728 | bytes 8388609 | tf_op jit(solution)/shard_map/jit(_where)/select_n | solution.py:213
  (274 shorter events, 247.0 us)
Async XLA Ops:
  18.8 39.2 %all-to-all-start = ((bf16[4,3,160,512]{3,2,1,0:T(8,128)(2,1)}), bf16[4,3,160,512]{3,2,1,0:T(8,128)(2,1)}, u32[]{:S(2)}, u32[]{:S(2)}) async-start(bf16[4,3,160,512]{3,2,1,0:T(8,128)(2,1)} %copy.414), calls=%async_computation | async-start | bytes 3932160 | tf_op jit(solution)/shard_map/all_to_all | solution.py:79
  83.1 52.9 %all-to-all-start.1 = ((bf16[16,15,64,128]{3,2,1,0:T(8,128)(2,1)}), bf16[16,15,64,128]{3,2,1,0:T(8,128)(2,1)}, u32[]{:S(2)}, u32[]{:S(2)}) async-start(bf16[16,15,64,128]{3,2,1,0:T(8,128)(2,1)} %bitcast.361), calls=%async_computation.1 | async-start | bytes 7864320 | tf_op jit(solution)/shard_map/all_to_all | solution.py:119
  91.2 127.4 %all-gather.3.cloned.1.call-start = ((), (), s32[]{:S(2)}) async-start(), calls=%async_computation.7 | async-start | bytes 3276800 | tf_op jit(solution)/shard_map/all_gather | solution.py:200
  136.0 95.5 %all-to-all-start.2 = ((bf16[16,15,64,128]{3,2,1,0:T(8,128)(2,1)}), bf16[16,15,64,128]{3,2,1,0:T(8,128)(2,1)}, u32[]{:S(2)}, u32[]{:S(2)}) async-start(bf16[16,15,64,128]{3,2,1,0:T(8,128)(2,1)} %bitcast.356), calls=%async_computation.2 | async-start | bytes 7864320 | tf_op jit(solution)/shard_map/all_to_all | solution.py:119
  146.9 38.2 %collective-permute-start.4 = (bf16[64,1024]{1,0:T(8,128)(2,1)S(1)}, bf16[64,1024]{1,0:T(8,128)(2,1)}, u32[]{:S(2)}, u32[]{:S(2)}) collective-permute-start(bf16[64,1024]{1,0:T(8,128)(2,1)S(1)} %get-tuple-element.107), channel_id=1, source_target_pairs={{0,16},{1,17},{2,18},{3,19},{64,80},{65,81},{66,82},{67,83}} | collective-permute-start | bytes 393224 | tf_op jit(solution)/shard_map/ppermute | solution.py:37
  150.7 37.4 %collective-permute-start.3 = (bf16[64,1024]{1,0:T(8,128)(2,1)S(1)}, bf16[64,1024]{1,0:T(8,128)(2,1)}, u32[]{:S(2)}, u32[]{:S(2)}) collective-permute-start(bf16[64,1024]{1,0:T(8,128)(2,1)S(1)} %get-tuple-element.107), channel_id=1, source_target_pairs={{0,32},{1,33},{2,34},{3,35},{64,96},{65,97},{66,98},{67,99}} | collective-permute-start | bytes 393224 | tf_op jit(solution)/shard_map/ppermute | solution.py:37
  153.5 34.6 %collective-permute-start.2 = (bf16[64,1024]{1,0:T(8,128)(2,1)S(1)}, bf16[64,1024]{1,0:T(8,128)(2,1)}, u32[]{:S(2)}, u32[]{:S(2)}) collective-permute-start(bf16[64,1024]{1,0:T(8,128)(2,1)S(1)} %get-tuple-element.107), channel_id=1, source_target_pairs={{0,48},{1,49},{2,50},{3,51},{64,112},{65,113},{66,114},{67,115}} | collective-permute-start | bytes 393224 | tf_op jit(solution)/shard_map/ppermute | solution.py:37
  188.2 27.8 %collective-permute-start.7 = (bf16[64,1024]{1,0:T(8,128)(2,1)S(1)}, bf16[64,1024]{1,0:T(8,128)(2,1)S(1)}, u32[]{:S(2)}, u32[]{:S(2)}) collective-permute-start(bf16[64,1024]{1,0:T(8,128)(2,1)S(1)} %select_select_fusion.1), channel_id=1, source_target_pairs={{0,4},{16,20},{32,36},{48,52},{1,5},{17,21},{33,37},{49,53},{2,6},... | collective-permute-start | bytes 393224 | tf_op jit(solution)/shard_map/ppermute | solution.py:37
  189.5 26.5 %collective-permute-start.6 = (bf16[64,1024]{1,0:T(8,128)(2,1)S(1)}, bf16[64,1024]{1,0:T(8,128)(2,1)S(1)}, u32[]{:S(2)}, u32[]{:S(2)}) collective-permute-start(bf16[64,1024]{1,0:T(8,128)(2,1)S(1)} %select_select_fusion.1), channel_id=1, source_target_pairs={{0,8},{16,24},{32,40},{48,56},{1,9},{17,25},{33,41},{49,57},{2,10}... | collective-permute-start | bytes 393224 | tf_op jit(solution)/shard_map/ppermute | solution.py:37
  257.4 95.5 %collective-permute-start.13 = (f32[64,1024]{1,0:T(8,128)}, f32[64,1024]{1,0:T(8,128)}, u32[]{:S(2)}, u32[]{:S(2)}) collective-permute-start(f32[64,1024]{1,0:T(8,128)} %reshape.631), channel_id=1, source_target_pairs={{12,0},{28,16},{44,32},{60,48},{13,1},{29,17},{45,33},{61,49},{14,... | collective-permute-start | bytes 786440 | tf_op jit(solution)/shard_map/ppermute | solution.py:53
  258.6 94.2 %collective-permute-start.12 = (f32[64,1024]{1,0:T(8,128)}, f32[64,1024]{1,0:T(8,128)}, u32[]{:S(2)}, u32[]{:S(2)}) collective-permute-start(f32[64,1024]{1,0:T(8,128)} %reshape.631), channel_id=1, source_target_pairs={{8,0},{24,16},{40,32},{56,48},{9,1},{25,17},{41,33},{57,49},{10,2}... | collective-permute-start | bytes 786440 | tf_op jit(solution)/shard_map/ppermute | solution.py:53
  259.9 92.9 %collective-permute-start.11 = (f32[64,1024]{1,0:T(8,128)}, f32[64,1024]{1,0:T(8,128)}, u32[]{:S(2)}, u32[]{:S(2)}) collective-permute-start(f32[64,1024]{1,0:T(8,128)} %reshape.631), channel_id=1, source_target_pairs={{4,0},{20,16},{36,32},{52,48},{5,1},{21,17},{37,33},{53,49},{6,2},... | collective-permute-start | bytes 786440 | tf_op jit(solution)/shard_map/ppermute | solution.py:53
  284.5 58.2 %all-to-all-start.5 = ((bf16[16,15,64,128]{3,2,1,0:T(8,128)(2,1)}), bf16[16,15,64,128]{3,2,1,0:T(8,128)(2,1)}, u32[]{:S(2)}, u32[]{:S(2)}) async-start(bf16[16,15,64,128]{3,2,1,0:T(8,128)(2,1)} %bitcast.362), calls=%async_computation.5 | async-start | bytes 7864320 | tf_op jit(solution)/shard_map/all_to_all | solution.py:318
  300.5 58.1 %collective-permute-start.19 = (f32[256,2048]{1,0:T(8,128)}, f32[256,2048]{1,0:T(8,128)}, u32[]{:S(2)}, u32[]{:S(2)}) collective-permute-start(f32[256,2048]{1,0:T(8,128)} %constant_dynamic-slice_fusion), channel_id=1, source_target_pairs={{0,64},{64,0},{1,65},{65,1},{2,66},{66,2},{3,67},{67,3},{4,68},{68... | collective-permute-start | bytes 6291464 | tf_op jit(solution)/shard_map/ppermute | solution.py:210
  342.7 147.2 %all-to-all-start.4 = ((bf16[16,15,64,128]{3,2,1,0:T(8,128)(2,1)}), bf16[16,15,64,128]{3,2,1,0:T(8,128)(2,1)}, u32[]{:S(2)}, u32[]{:S(2)}) async-start(bf16[16,15,64,128]{3,2,1,0:T(8,128)(2,1)} %bitcast.357), calls=%async_computation.4 | async-start | bytes 7864320 | tf_op jit(solution)/shard_map/all_to_all | solution.py:318
  351.3 133.4 %all-reduce.5.cloned.1.call-start = ((), (), s32[]{:S(2)}) async-start(), calls=%async_computation.8 | async-start | bytes 4194304 | tf_op jit(solution)/shard_map/psum | solution.py:211
  354.7 50.8 %collective-permute-start.16 = (f32[64,1024]{1,0:T(8,128)}, f32[64,1024]{1,0:T(8,128)}, u32[]{:S(2)}, u32[]{:S(2)}) collective-permute-start(f32[64,1024]{1,0:T(8,128)} %add_add_fusion), channel_id=1, source_target_pairs={{48,0},{49,1},{50,2},{51,3},{112,64},{113,65},{114,66},{115,67}} | collective-permute-start | bytes 786440 | tf_op jit(solution)/shard_map/ppermute | solution.py:53
  356.0 49.5 %collective-permute-start.15 = (f32[64,1024]{1,0:T(8,128)}, f32[64,1024]{1,0:T(8,128)}, u32[]{:S(2)}, u32[]{:S(2)}) collective-permute-start(f32[64,1024]{1,0:T(8,128)} %add_add_fusion), channel_id=1, source_target_pairs={{32,0},{33,1},{34,2},{35,3},{96,64},{97,65},{98,66},{99,67}} | collective-permute-start | bytes 786440 | tf_op jit(solution)/shard_map/ppermute | solution.py:53
  357.3 48.2 %collective-permute-start.14 = (f32[64,1024]{1,0:T(8,128)}, f32[64,1024]{1,0:T(8,128)}, u32[]{:S(2)}, u32[]{:S(2)}) collective-permute-start(f32[64,1024]{1,0:T(8,128)} %add_add_fusion), channel_id=1, source_target_pairs={{16,0},{17,1},{18,2},{19,3},{80,64},{81,65},{82,66},{83,67}} | collective-permute-start | bytes 786440 | tf_op jit(solution)/shard_map/ppermute | solution.py:53
  411.4 27.4 %collective-permute-start.18 = (bf16[64,1024]{1,0:T(8,128)(2,1)S(1)}, bf16[64,1024]{1,0:T(8,128)(2,1)S(1)}, u32[]{:S(2)}, u32[]{:S(2)}) collective-permute-start(bf16[64,1024]{1,0:T(8,128)(2,1)S(1)} %concatenate.48), channel_id=1, source_target_pairs={{4,0},{8,4},{12,8},{16,12},{20,16},{24,20},{28,24},{32,28},{36,32}... | collective-permute-start | bytes 393224 | tf_op jit(solution)/shard_map/ppermute | solution.py:20
  422.7 93.6 %collective-permute-start.8 = (f32[160,2048]{1,0:T(8,128)}, f32[160,2048]{1,0:T(8,128)}, u32[]{:S(2)}, u32[]{:S(2)}) collective-permute-start(f32[160,2048]{1,0:T(8,128)} %get-tuple-element.83), channel_id=1, source_target_pairs={{0,1},{1,2},{2,3},{3,0},{4,5},{5,6},{6,7},{7,4},{8,9},{9,10},{10,1... | collective-permute-start | bytes 3932168 | tf_op jit(solution)/shard_map/ppermute | solution.py:198
  426.8 89.5 %collective-permute-start.10 = (f32[160,2048]{1,0:T(8,128)}, f32[160,2048]{1,0:T(8,128)}, u32[]{:S(2)}, u32[]{:S(2)}) collective-permute-start(f32[160,2048]{1,0:T(8,128)} %get-tuple-element.84), channel_id=1, source_target_pairs={{0,3},{1,0},{2,1},{3,2},{4,7},{5,4},{6,5},{7,6},{8,11},{9,8},{10,9... | collective-permute-start | bytes 3932168 | tf_op jit(solution)/shard_map/ppermute | solution.py:198
  426.8 89.5 %collective-permute-start.9 = (f32[160,2048]{1,0:T(8,128)}, f32[160,2048]{1,0:T(8,128)}, u32[]{:S(2)}, u32[]{:S(2)}) collective-permute-start(f32[160,2048]{1,0:T(8,128)} %get-tuple-element.85), channel_id=1, source_target_pairs={{0,2},{1,3},{2,0},{3,1},{4,6},{5,7},{6,4},{7,5},{8,10},{9,11},{10,... | collective-permute-start | bytes 3932168 | tf_op jit(solution)/shard_map/ppermute | solution.py:198
  487.9 45.5 %collective-permute-start.20 = (f32[256,2048]{1,0:T(8,128)}, f32[256,2048]{1,0:T(8,128)}, u32[]{:S(2)}, u32[]{:S(2)}) collective-permute-start(f32[256,2048]{1,0:T(8,128)} %broadcast_multiply_fusion), channel_id=1, source_target_pairs={{0,64},{64,0},{1,65},{65,1},{2,66},{66,2},{3,67},{67,3},{4,68},{68... | collective-permute-start | bytes 6291464 | tf_op jit(solution)/shard_map/ppermute | solution.py:212
  (39 other events, 457.6 us)
Sparse Core Ops, SparseCore 0:
  93.6 41.8 all-gather.2
  362.6 121.9 all-reduce.4

commit v6 on v4

--- a/solution.py
+++ b/solution.py
@@ -61,9 +61,38 @@
     head_of = jnp.arange(requests.shape[0], dtype=jnp.int32) % head_count
     owners = requests // block_count
     offsets = requests % block_count
-    one_hot = (owners[:, None] == jnp.arange(seq_count, dtype=jnp.int32)[None, :]).astype(jnp.int32)
-    position = jnp.sum(one_hot * (jnp.cumsum(one_hot, axis=0) - 1), axis=1)
+    one_hot = (owners[:, None] == jnp.arange(seq_count, dtype=jnp.int32)[None, :]).astype(
+        jnp.bfloat16
+    )
+    count = requests.shape[0]
+    lower = (
+        jnp.arange(count, dtype=jnp.int32)[:, None] >= jnp.arange(count, dtype=jnp.int32)[None, :]
+    ).astype(jnp.bfloat16)
+    running = jnp.dot(lower, one_hot, preferred_element_type=jnp.float32)
+    position = jnp.sum(one_hot.astype(jnp.float32) * (running - 1.0), axis=1).astype(jnp.int32)
     return owners, position, offsets * head_count + head_of
+
+
+def gather_all(block, axis, radix=4):
+    count = lax.axis_size(axis)
+    if count != radix * radix:
+        return lax.all_gather(block, axis, axis=0, tiled=False)
+    index = lax.axis_index(axis)
+    for stride in (1, radix):
+        place = (index // stride) % radix
+        pieces = [block]
+        for m in range(1, radix):
+            pairs = [
+                (i, i - ((i // stride) % radix) * stride + (((i // stride) % radix + m) % radix) * stride)
+                for i in range(count)
+            ]
+            pieces.append(lax.ppermute(block, axis, pairs))
+        pieces = jnp.stack(pieces)
+        order = (place - jnp.arange(radix, dtype=jnp.int32)) % radix
+        block = jnp.take(pieces, order, axis=0)
+        if stride > 1:
+            block = block.reshape((radix * radix,) + block.shape[2:])
+    return block
 
 
 def per_device(queries, key_rows, values, rand_blocks, out_weight, cotangent):
@@ -92,7 +121,7 @@
         rand_blocks, block_count, head_count, seq_count, capacity
     )
     slot_of = owners * capacity + position
-    every_block = lax.all_gather(rand_blocks, "seq", axis=0, tiled=False)
+    every_block = gather_all(rand_blocks, "seq")
     all_owners, all_position, all_codes = jax.vmap(
         lambda r: request_slots(r, block_count, head_count, seq_count, capacity)
     )(every_block)

time: 531 us -> 521 us (0.981)
  blocking collectives: 22.3 us -> 0 us
  waiting for transfers between devices: 156 us -> 169 us
  other arithmetic: 71.3 us -> 61.6 us
  starting transfers between devices: 79.2 us -> 87.2 us
    all_gather x1 -> x0, blocking collectives: 22.3 us -> none  [per_device(): every_block = lax.all_gather(rand_blocks, 'seq', axis=0, tiled=False)]
    all_to_all x1, waiting for transfers between devices: 0.01 us -> 12.4 us  [per_device(): lax.all_to_all(stacked, 'head', split_axis=0, concat_axis=0, tiled=True)]
    another operation x10 -> x4, other arithmetic: 14.3 us -> 4.45 us
    ppermute x0 -> x6, starting transfers between devices: none -> 8.96 us  [gather_all(): pieces.append(lax.ppermute(block, axis, pairs))]
    unnamed x89 -> x88, local copies, waits for them, and re-layouts: 29.1 us -> 29 us
  transfers between devices with their start and end apart: 28 -> 34, of which waited for: 8 -> 12; matrix products, arithmetic and copies ran while one was open for 37% -> 39% of each run, Pallas kernels for 0% -> 0%
where the time goes in v6:
time: 521 us; the launch traced here: 511 us
  waiting for transfers between devices  169 us (32%)
  local copies, waits for them, and re-layouts  106 us (20%)
  starting transfers between devices  87.2 us (17%)
  matrix products  72.3 us (14%)
  other arithmetic  61.6 us (12%)
  between operations  15.3 us (3%)
    ppermute x6, waiting for transfers between devices, reduce_to_first(): total = total + lax.ppermute(block, axis, pairs)  39.1 us
    all_to_all x2, waiting for transfers between devices, to_owners(): lax.all_to_all(jnp.transpose(rows, (1, 0, 2, 3)), 'head', split_axis=0, c...  34.2 us
    unnamed x88, local copies, waits for them, and re-layouts  29 us
    ppermute x6, waiting for transfers between devices, broadcast_first(): got = lax.ppermute(block, axis, pairs)  27.6 us
    all_to_all x2, waiting for transfers between devices, fetch(): lax.all_to_all(served, 'seq', split_axis=0, concat_axis=0, tiled=True)  26.5 us
    all_to_all x2, waiting for transfers between devices, give_back(): lax.all_to_all(outgoing, 'seq', split_axis=0, concat_axis=0, tiled=True)  21.3 us
    all_to_all x2, starting transfers between devices, fetch(): lax.all_to_all(served, 'seq', split_axis=0, concat_axis=0, tiled=True)  14.9 us
    ppermute x6, starting transfers between devices, broadcast_first(): got = lax.ppermute(block, axis, pairs)  14.6 us
  transfers between devices with their start and end apart: 34, of which 12 were waited for; matrix products, arithmetic and copies ran while one was open for 39% of the time, Pallas kernels for 0%

profile of v6, /device:TPU:1, one launch (start us, length us, event | category | flops | bytes accessed | tf_op | source)
XLA Modules:
  0.0 511.1 jit_solution(9724937003704250488)
XLA Ops:
  14.6 5.3 %reshape.710 = bf16[3,160,4,512]{3,2,1,0:T(4,128)(2,1)} reshape(bf16[3,160,2048]{2,1,0:T(8,128)(2,1)} %pad_maximum_fusion.1) | data formatting | bytes 3932160 | tf_op jit(solution)/shard_map/reshape | solution.py:107
  38.8 12.4 %all-to-all-done = bf16[4,3,160,512]{3,2,1,0:T(8,128)(2,1)} async-done(((bf16[4,3,160,512]{3,2,1,0:T(8,128)(2,1)}), bf16[4,3,160,512]{3,2,1,0:T(8,128)(2,1)}, u32[]{:S(2)}, u32[]{:S(2)}) %all-to-all-start) | async-done | bytes 1966112 | tf_op jit(solution)/shard_map/all_to_all | solution.py:108
  64.3 4.9 pad_maximum_fusion.5
  77.0 9.1 %all-to-all-start.1 = ((bf16[16,15,64,128]{3,2,1,0:T(8,128)(2,1)}), bf16[16,15,64,128]{3,2,1,0:T(8,128)(2,1)}, u32[]{:S(2)}, u32[]{:S(2)}) async-start(bf16[16,15,64,128]{3,2,1,0:T(8,128)(2,1)} %bitcast.335), calls=%async_computation.1 | async-start | bytes 7864320 | tf_op jit(solution)/shard_map/all_to_all | solution.py:148
  87.8 5.1 collective-permute-start.2
  102.7 27.6 %collective-permute-done.2 = bf16[64,1024]{1,0:T(8,128)(2,1)} collective-permute-done((bf16[64,1024]{1,0:T(8,128)(2,1)S(1)}, bf16[64,1024]{1,0:T(8,128)(2,1)}, u32[]{:S(2)}, u32[]{:S(2)}) %collective-permute-start.2) | collective-permute-done | bytes 131104 | tf_op jit(solution)/shard_map/ppermute | solution.py:37
  143.7 4.9 pad_maximum_fusion
  156.1 5.8 %all-to-all-start.2 = ((bf16[16,15,64,128]{3,2,1,0:T(8,128)(2,1)}), bf16[16,15,64,128]{3,2,1,0:T(8,128)(2,1)}, u32[]{:S(2)}, u32[]{:S(2)}) async-start(bf16[16,15,64,128]{3,2,1,0:T(8,128)(2,1)} %bitcast.337), calls=%async_computation.2 | async-start | bytes 7864320 | tf_op jit(solution)/shard_map/all_to_all | solution.py:148
  162.0 5.0 select_reduce_fusion
  176.5 4.8 fusion.52
  191.6 26.5 %all-to-all-done.2 = bf16[16,15,64,128]{3,2,1,0:T(8,128)(2,1)} async-done(((bf16[16,15,64,128]{3,2,1,0:T(8,128)(2,1)}), bf16[16,15,64,128]{3,2,1,0:T(8,128)(2,1)}, u32[]{:S(2)}, u32[]{:S(2)}) %all-to-all-start.2) | async-done | bytes 3932192 | tf_op jit(solution)/shard_map/all_to_all | solution.py:148
  218.1 4.8 fusion.55
  267.0 7.5 %all-to-all-start.5 = ((bf16[16,15,64,128]{3,2,1,0:T(8,128)(2,1)}), bf16[16,15,64,128]{3,2,1,0:T(8,128)(2,1)}, u32[]{:S(2)}, u32[]{:S(2)}) async-start(bf16[16,15,64,128]{3,2,1,0:T(8,128)(2,1)} %bitcast.338), calls=%async_computation.6 | async-start | bytes 7864320 | tf_op jit(solution)/shard_map/all_to_all | solution.py:341
  274.9 5.1 multiply_convert_fusion.1
  316.8 21.3 %all-to-all-done.5 = bf16[16,15,64,128]{3,2,1,0:T(8,128)(2,1)} async-done(((bf16[16,15,64,128]{3,2,1,0:T(8,128)(2,1)}), bf16[16,15,64,128]{3,2,1,0:T(8,128)(2,1)}, u32[]{:S(2)}, u32[]{:S(2)}) %all-to-all-start.5) | async-done | bytes 3932192 | tf_op jit(solution)/shard_map/all_to_all | solution.py:341
  338.1 4.7 all-to-all-start.4
  342.9 4.8 fusion.19
  356.4 39.0 %collective-permute-done.19 = f32[64,1024]{1,0:T(8,128)S(1)} collective-permute-done((f32[64,1024]{1,0:T(8,128)S(1)}, f32[64,1024]{1,0:T(8,128)S(1)}, u32[]{:S(2)}, u32[]{:S(2)}) %collective-permute-start.19) | collective-permute-done | bytes 262176 | tf_op jit(solution)/shard_map/ppermute | solution.py:53
  403.3 4.6 collective-permute-start.20
  427.6 6.1 %fusion.59 = f32[10,4,64,1,128]{4,0,2,1,3:T(8,128)} fusion(s32[10,4]{0,1:T(4,128)S(1)} %multiply_add_fusion, s32[240]{0:T(256)S(1)} %sub.161, bf16[30,8,64,128]{3,2,1,0:T(8,128)(2,1)} %bitcast.163), kind=kOutput, calls=%fused_computation.90 | convolution fusion | flops 157296000 | bytes 5244000 | tf_op jit(solution)/shard_map/dot_general | solution.py:342
  443.8 4.8 fusion.58
  453.5 8.8 %all-to-all-done.3 = bf16[4,1,160,512]{3,2,1,0:T(8,128)(2,1)} async-done(((bf16[4,1,160,512]{3,2,1,0:T(8,128)(2,1)}), bf16[4,1,160,512]{3,2,1,0:T(8,128)(2,1)}, u32[]{:S(2)}, u32[]{:S(2)}) %all-to-all-start.3) | async-done | bytes 655392 | tf_op jit(solution)/shard_map/all_to_all | solution.py:356
  467.8 25.4 %all-to-all-done.6 = bf16[4,2,160,512]{3,2,1,0:T(8,128)(2,1)S(1)} async-done(((bf16[4,2,160,512]{3,2,1,0:T(8,128)(2,1)}), bf16[4,2,160,512]{3,2,1,0:T(8,128)(2,1)S(1)}, u32[]{:S(2)}, u32[]{:S(2)}) %all-to-all-start.6) | async-done | bytes 1310752 | tf_op jit(solution)/shard_map/all_to_all | solution.py:356
  495.2 6.7 %maximum_select_fusion = f32[512,2048]{1,0:T(8,128)} fusion(f32[256,2048]{1,0:T(8,128)} %collective-permute-done.23, f32[256,2048]{1,0:T(8,128)} %broadcast_multiply_fusion, pred[]{:T(512)S(6)} %eq.171), kind=kLoop, calls=%fused_computation.18 | loop fusion | flops 3145728 | bytes 8388609 | tf_op jit(solution)/shard_map/jit(_where)/select_n | solution.py:236
  (287 shorter events, 240.7 us)
Async XLA Ops:
  7.2 20.9 %collective-permute-start.10 = (s32[10,4,4]{0,2,1:T(4,128)}, s32[10,4,4]{0,2,1:T(4,128)S(1)}, u32[]{:S(2)}, u32[]{:S(2)}) collective-permute-start(s32[10,4,4]{0,2,1:T(4,128)} %param.21), channel_id=1, source_target_pairs={{0,12},{4,0},{8,4},{12,8},{16,28},{20,16},{24,20},{28,24},{32,44},... | collective-permute-start | bytes 1928 | tf_op jit(solution)/shard_map/ppermute | solution.py:89
  23.1 28.1 %all-to-all-start = ((bf16[4,3,160,512]{3,2,1,0:T(8,128)(2,1)}), bf16[4,3,160,512]{3,2,1,0:T(8,128)(2,1)}, u32[]{:S(2)}, u32[]{:S(2)}) async-start(bf16[4,3,160,512]{3,2,1,0:T(8,128)(2,1)} %copy.355), calls=%async_computation | async-start | bytes 3932160 | tf_op jit(solution)/shard_map/all_to_all | solution.py:108
  77.0 79.1 %all-to-all-start.1 = ((bf16[16,15,64,128]{3,2,1,0:T(8,128)(2,1)}), bf16[16,15,64,128]{3,2,1,0:T(8,128)(2,1)}, u32[]{:S(2)}, u32[]{:S(2)}) async-start(bf16[16,15,64,128]{3,2,1,0:T(8,128)(2,1)} %bitcast.335), calls=%async_computation.1 | async-start | bytes 7864320 | tf_op jit(solution)/shard_map/all_to_all | solution.py:148
  86.0 84.5 %all-gather.2.cloned.1.call-start = ((), (), s32[]{:S(2)}) async-start(), calls=%async_computation.9 | async-start | bytes 3276800 | tf_op jit(solution)/shard_map/all_gather | solution.py:223
  87.8 42.5 %collective-permute-start.2 = (bf16[64,1024]{1,0:T(8,128)(2,1)S(1)}, bf16[64,1024]{1,0:T(8,128)(2,1)}, u32[]{:S(2)}, u32[]{:S(2)}) collective-permute-start(bf16[64,1024]{1,0:T(8,128)(2,1)S(1)} %get-tuple-element.104), channel_id=1, source_target_pairs={{0,48},{1,49},{2,50},{3,51},{64,112},{65,113},{66,114},{67,115}} | collective-permute-start | bytes 393224 | tf_op jit(solution)/shard_map/ppermute | solution.py:37
  92.9 37.4 %collective-permute-start.3 = (bf16[64,1024]{1,0:T(8,128)(2,1)S(1)}, bf16[64,1024]{1,0:T(8,128)(2,1)}, u32[]{:S(2)}, u32[]{:S(2)}) collective-permute-start(bf16[64,1024]{1,0:T(8,128)(2,1)S(1)} %get-tuple-element.104), channel_id=1, source_target_pairs={{0,32},{1,33},{2,34},{3,35},{64,96},{65,97},{66,98},{67,99}} | collective-permute-start | bytes 393224 | tf_op jit(solution)/shard_map/ppermute | solution.py:37
  94.8 35.5 %collective-permute-start.4 = (bf16[64,1024]{1,0:T(8,128)(2,1)S(1)}, bf16[64,1024]{1,0:T(8,128)(2,1)}, u32[]{:S(2)}, u32[]{:S(2)}) collective-permute-start(bf16[64,1024]{1,0:T(8,128)(2,1)S(1)} %get-tuple-element.104), channel_id=1, source_target_pairs={{0,16},{1,17},{2,18},{3,19},{64,80},{65,81},{66,82},{67,83}} | collective-permute-start | bytes 393224 | tf_op jit(solution)/shard_map/ppermute | solution.py:37
  131.0 36.0 %collective-permute-start.5 = (bf16[64,1024]{1,0:T(8,128)(2,1)}, bf16[64,1024]{1,0:T(8,128)(2,1)S(1)}, u32[]{:S(2)}, u32[]{:S(2)}) collective-permute-start(bf16[64,1024]{1,0:T(8,128)(2,1)} %select_select_fusion.1), channel_id=1, source_target_pairs={{0,12},{16,28},{32,44},{48,60},{1,13},{17,29},{33,45},{49,61},{2,1... | collective-permute-start | bytes 393224 | tf_op jit(solution)/shard_map/ppermute | solution.py:37
  132.3 34.7 %collective-permute-start.6 = (bf16[64,1024]{1,0:T(8,128)(2,1)}, bf16[64,1024]{1,0:T(8,128)(2,1)}, u32[]{:S(2)}, u32[]{:S(2)}) collective-permute-start(bf16[64,1024]{1,0:T(8,128)(2,1)} %select_select_fusion.1), channel_id=1, source_target_pairs={{0,8},{16,24},{32,40},{48,56},{1,9},{17,25},{33,41},{49,57},{2,10}... | collective-permute-start | bytes 393224 | tf_op jit(solution)/shard_map/ppermute | solution.py:37
  134.3 32.7 %collective-permute-start.7 = (bf16[64,1024]{1,0:T(8,128)(2,1)}, bf16[64,1024]{1,0:T(8,128)(2,1)}, u32[]{:S(2)}, u32[]{:S(2)}) collective-permute-start(bf16[64,1024]{1,0:T(8,128)(2,1)} %select_select_fusion.1), channel_id=1, source_target_pairs={{0,4},{16,20},{32,36},{48,52},{1,5},{17,21},{33,37},{49,53},{2,6},... | collective-permute-start | bytes 393224 | tf_op jit(solution)/shard_map/ppermute | solution.py:37
  156.1 62.0 %all-to-all-start.2 = ((bf16[16,15,64,128]{3,2,1,0:T(8,128)(2,1)}), bf16[16,15,64,128]{3,2,1,0:T(8,128)(2,1)}, u32[]{:S(2)}, u32[]{:S(2)}) async-start(bf16[16,15,64,128]{3,2,1,0:T(8,128)(2,1)} %bitcast.337), calls=%async_computation.2 | async-start | bytes 7864320 | tf_op jit(solution)/shard_map/all_to_all | solution.py:148
  161.9 271.8 %all-reduce.3.cloned.1.call-start = ((), (), s32[]{:S(2)}) async-start(), calls=%async_computation.10 | async-start | bytes 4194304 | tf_op jit(solution)/shard_map/psum | solution.py:234
  244.1 105.7 %collective-permute-start.16 = (f32[64,1024]{1,0:T(8,128)}, f32[64,1024]{1,0:T(8,128)}, u32[]{:S(2)}, u32[]{:S(2)}) collective-permute-start(f32[64,1024]{1,0:T(8,128)} %reshape.724), channel_id=1, source_target_pairs={{12,0},{28,16},{44,32},{60,48},{13,1},{29,17},{45,33},{61,49},{14,... | collective-permute-start | bytes 786440 | tf_op jit(solution)/shard_map/ppermute | solution.py:53
  245.3 104.5 %collective-permute-start.15 = (f32[64,1024]{1,0:T(8,128)}, f32[64,1024]{1,0:T(8,128)}, u32[]{:S(2)}, u32[]{:S(2)}) collective-permute-start(f32[64,1024]{1,0:T(8,128)} %reshape.724), channel_id=1, source_target_pairs={{8,0},{24,16},{40,32},{56,48},{9,1},{25,17},{41,33},{57,49},{10,2}... | collective-permute-start | bytes 786440 | tf_op jit(solution)/shard_map/ppermute | solution.py:53
  246.6 103.2 %collective-permute-start.14 = (f32[64,1024]{1,0:T(8,128)}, f32[64,1024]{1,0:T(8,128)}, u32[]{:S(2)}, u32[]{:S(2)}) collective-permute-start(f32[64,1024]{1,0:T(8,128)} %reshape.724), channel_id=1, source_target_pairs={{4,0},{20,16},{36,32},{52,48},{5,1},{21,17},{37,33},{53,49},{6,2},... | collective-permute-start | bytes 786440 | tf_op jit(solution)/shard_map/ppermute | solution.py:53
  267.0 71.1 %all-to-all-start.5 = ((bf16[16,15,64,128]{3,2,1,0:T(8,128)(2,1)}), bf16[16,15,64,128]{3,2,1,0:T(8,128)(2,1)}, u32[]{:S(2)}, u32[]{:S(2)}) async-start(bf16[16,15,64,128]{3,2,1,0:T(8,128)(2,1)} %bitcast.338), calls=%async_computation.6 | async-start | bytes 7864320 | tf_op jit(solution)/shard_map/all_to_all | solution.py:341
  274.5 227.4 %reduce-scatter.2.cloned.1.call-start = ((), (), s32[]{:S(2)}) async-start(), calls=%async_computation.8 | async-start | bytes 6553600 | tf_op jit(solution)/shard_map/reduce_scatter | solution.py:217
  338.1 101.2 %all-to-all-start.4 = ((bf16[16,15,64,128]{3,2,1,0:T(8,128)(2,1)}), bf16[16,15,64,128]{3,2,1,0:T(8,128)(2,1)}, u32[]{:S(2)}, u32[]{:S(2)}) async-start(bf16[16,15,64,128]{3,2,1,0:T(8,128)(2,1)} %bitcast.336), calls=%async_computation.5 | async-start | bytes 7864320 | tf_op jit(solution)/shard_map/all_to_all | solution.py:341
  351.0 44.5 %collective-permute-start.19 = (f32[64,1024]{1,0:T(8,128)S(1)}, f32[64,1024]{1,0:T(8,128)S(1)}, u32[]{:S(2)}, u32[]{:S(2)}) collective-permute-start(f32[64,1024]{1,0:T(8,128)S(1)} %add_add_fusion), channel_id=1, source_target_pairs={{48,0},{49,1},{50,2},{51,3},{112,64},{113,65},{114,66},{115,67}} | collective-permute-start | bytes 786440 | tf_op jit(solution)/shard_map/ppermute | solution.py:53
  352.3 43.2 %collective-permute-start.18 = (f32[64,1024]{1,0:T(8,128)S(1)}, f32[64,1024]{1,0:T(8,128)S(1)}, u32[]{:S(2)}, u32[]{:S(2)}) collective-permute-start(f32[64,1024]{1,0:T(8,128)S(1)} %add_add_fusion), channel_id=1, source_target_pairs={{32,0},{33,1},{34,2},{35,3},{96,64},{97,65},{98,66},{99,67}} | collective-permute-start | bytes 786440 | tf_op jit(solution)/shard_map/ppermute | solution.py:53
  353.6 41.9 %collective-permute-start.17 = (f32[64,1024]{1,0:T(8,128)S(1)}, f32[64,1024]{1,0:T(8,128)S(1)}, u32[]{:S(2)}, u32[]{:S(2)}) collective-permute-start(f32[64,1024]{1,0:T(8,128)S(1)} %add_add_fusion), channel_id=1, source_target_pairs={{16,0},{17,1},{18,2},{19,3},{80,64},{81,65},{82,66},{83,67}} | collective-permute-start | bytes 786440 | tf_op jit(solution)/shard_map/ppermute | solution.py:53
  437.0 58.2 %collective-permute-start.23 = (f32[256,2048]{1,0:T(8,128)}, f32[256,2048]{1,0:T(8,128)}, u32[]{:S(2)}, u32[]{:S(2)}) collective-permute-start(f32[256,2048]{1,0:T(8,128)} %broadcast_multiply_fusion), channel_id=1, source_target_pairs={{0,64},{64,0},{1,65},{65,1},{2,66},{66,2},{3,67},{67,3},{4,68},{68... | collective-permute-start | bytes 6291464 | tf_op jit(solution)/shard_map/ppermute | solution.py:235
  439.4 22.9 %all-to-all-start.3 = ((bf16[4,1,160,512]{3,2,1,0:T(8,128)(2,1)}), bf16[4,1,160,512]{3,2,1,0:T(8,128)(2,1)}, u32[]{:S(2)}, u32[]{:S(2)}) async-start(bf16[4,1,160,512]{3,2,1,0:T(8,128)(2,1)} %bitcast.57), calls=%async_computation.4 | async-start | bytes 1310720 | tf_op jit(solution)/shard_map/all_to_all | solution.py:356
  462.3 31.0 %all-to-all-start.6 = ((bf16[4,2,160,512]{3,2,1,0:T(8,128)(2,1)}), bf16[4,2,160,512]{3,2,1,0:T(8,128)(2,1)S(1)}, u32[]{:S(2)}, u32[]{:S(2)}) async-start(bf16[4,2,160,512]{3,2,1,0:T(8,128)(2,1)} %copy.422), calls=%async_computation.7 | async-start | bytes 2621440 | tf_op jit(solution)/shard_map/all_to_all | solution.py:356
  (50 other events, 410.9 us)
Sparse Core Ops, SparseCore 0:
  88.5 38.0 all-gather.1
  258.1 157.0 all-reduce.2
  417.6 71.1 reduce-scatter.1
